TPU v7x, 256 devices: a whole 4x4x8 slice. The times are simulated.
256 devices in a mesh: section: 4 (over x), shard: 16 (over z, core), tensor: 4 (over y).
Axes of the slice: x: 4, y: 4, z: 8, core: 2. Of those that a mesh axis runs over, the one named last changes fastest.
Arguments:
- grad_terms: float32 [4, 16, 5120, 1280], P('section', 'shard', 'tensor'), may hold values from -5 to 5
- weights: bfloat16 [4, 4, 1280, 1280], P('section', 'tensor', 'shard'), may hold values from -4 to 4
- basis: float32 [4, 1280, 256], P('section'), may hold values from -5 to 5
- first_moment: float32 [4, 4, 1280, 256], P('section', 'tensor', 'shard'), may hold values from -4 to 4
- second_moment: float32 [4, 4, 1280, 256], P('section', 'tensor', 'shard'), may hold values from 0.1 to 2
Outputs:
- new_weights: bfloat16 [4, 4, 1280, 1280], P('section', 'tensor', 'shard')
- new_first: float32 [4, 4, 1280, 256], P('section', 'tensor', 'shard')
- new_second: float32 [4, 4, 1280, 256], P('section', 'tensor', 'shard')
- new_basis: float32 [4, 1280, 256], P('section')
All inputs are finite; a program needn't handle non-finite values.
Results may differ from a plain program's by a relative error of at most 0.001.
Values sent between devices are 32-bit elements; how exact they have to be, the bound alone decides.
No kernel may reach another device: no remote copies, remote signals or barrier semaphores. Data moves between devices by JAX's collectives and lax.ppermute only.
A program may use at most 64 MiB of HBM per device.

v0:
```python
import math

import jax
import jax.numpy as jnp
from jax import lax
from jax.sharding import PartitionSpec as P

NS_STEPS = 5


def matmul(left, right):
    return jnp.dot(left, right, precision=lax.Precision.HIGHEST, preferred_element_type=jnp.float32)


def inner_rows(left, right):
    return lax.dot_general(
        left,
        right,
        (((0,), (0,)), ((), ())),
        precision=lax.Precision.HIGHEST,
        preferred_element_type=jnp.float32,
    )


def local_gram(iterate):
    return inner_rows(iterate, iterate)


def newton_steps(power_part, gram_fn):
    gram_now = gram_fn(power_part)
    scaling = lax.rsqrt(jnp.trace(gram_now) + 1e-06)
    iterate = power_part * scaling
    gram_now = gram_now * (scaling * scaling)
    for sweep in range(NS_STEPS):
        iterate = 1.5 * iterate - 0.5 * matmul(iterate, gram_now)
        if sweep + 1 < NS_STEPS:
            gram_now = gram_fn(iterate)
    return iterate


def per_device(grad_terms, weights, basis, first_moment, second_moment):
    gradient = grad_terms[0, 0]
    basis_now = basis[0]
    root_width = math.sqrt(basis_now.shape[0])
    grad_rows = lax.psum_scatter(gradient, "shard", scatter_dimension=0, tiled=True)
    low_rank = matmul(grad_rows, basis_now) / root_width
    power_part = inner_rows(grad_rows, low_rank)
    moment_one = 0.9 * first_moment[0, 0] + 0.1 * low_rank
    moment_two = 0.95 * second_moment[0, 0] + 0.05 * low_rank * low_rank
    direction = moment_one / (jnp.sqrt(moment_two) + 1e-08)
    update = lax.dot_general(
        direction,
        basis_now,
        (((1,), (1,)), ((), ())),
        precision=lax.Precision.HIGHEST,
        preferred_element_type=jnp.float32,
    )
    stepped = weights[0, 0].astype(jnp.float32) - 0.5 * update / root_width
    normed = stepped * lax.rsqrt(jnp.mean(stepped * stepped, axis=1, keepdims=True) + 1e-06)
    new_weights = normed.astype(jnp.bfloat16)
    power = lax.psum(power_part, ("shard", "tensor"))
    iterate = newton_steps(power, local_gram)
    new_basis = iterate * root_width
    return (
        new_weights[None, None],
        moment_one[None, None],
        moment_two[None, None],
        new_basis[None],
    )


def solution(mesh):
    return jax.shard_map(
        per_device,
        mesh=mesh,
        in_specs=(
            P("section", "shard", "tensor", None),
            P("section", "tensor", "shard", None),
            P("section", None, None),
            P("section", "tensor", "shard", None),
            P("section", "tensor", "shard", None),
        ),
        out_specs=(
            P("section", "tensor", "shard", None),
            P("section", "tensor", "shard", None),
            P("section", "tensor", "shard", None),
            P("section", None, None),
        ),
        check_vma=False,
    )
```

profile of v0, /device:TPU:1, one launch (start us, length us, event | category | flops | bytes accessed | tf_op | source)
XLA Modules:
  0.0 296.4 jit_solution(4766356547006104338)
XLA Ops:
  7.2 0.0 copy-start
  7.2 0.0 reduce-scatter.2.cloned.1.call-start
  7.2 0.7 reduce-scatter.2.cloned.1.call-update
  7.9 0.0 all-reduce.2.cloned.1.call-start
  8.0 70.8 %reduce-scatter.2.cloned.1.call-done = f32[80,1280]{1,0:T(8,128)} async-done(((f32[1280,1280]{1,0:T(8,128)}), f32[80,1280]{1,0:T(8,128)}) %reduce-scatter.2.cloned.1.call-update) | async-done | bytes 409616 | tf_op jit(solution)/shard_map/reduce_scatter | solution.py:45
  78.8 0.0 copy-done
  78.8 0.0 copy-start.2
  78.8 1.9 fusion.9
  80.7 0.0 copy-done.2
  80.7 0.0 copy-start.3
  80.7 0.0 copy-start.4
  80.7 2.3 convolution_bitcast_fusion
  83.0 0.0 all-reduce.2.cloned.1.call-update
  83.0 0.0 copy-done.3
  83.0 0.0 copy-done.4
  83.0 0.7 fusion.23
  83.7 0.2 copy-done.5
  83.9 1.5 multiply_reduce_fusion
  85.4 0.8 fusion.14
  86.2 185.4 %all-reduce.2.cloned.1.call-done = f32[1280,256]{0,1:T(8,128)} async-done(((f32[1280,256]{0,1:T(8,128)}), f32[1280,256]{0,1:T(8,128)}) %all-reduce.2.cloned.1.call-update) | async-done | bytes 1310736 | tf_op jit(solution)/shard_map/psum | solution.py:61
  271.5 3.7 %select_reduce_fusion = (f32[]{:T(128)}, f32[256,256]{1,0:T(8,128)S(1)}) fusion(f32[1280,256]{0,1:T(8,128)} %all-reduce.2.cloned.1.call-done), kind=kOutput, calls=%fused_computation.23 | convolution fusion | flops 1006829568 | bytes 1572868 | tf_op jit(solution)/shard_map/dot_general | solution.py:16
  276.0 0.0 copy-done.1
  276.0 1.4 fusion.5
  277.4 1.2 fusion.31
  278.6 1.4 fusion.4
  280.0 1.2 fusion.32
  281.2 1.4 fusion.3
  282.6 1.4 fusion.33
  284.1 1.4 fusion.2
  285.4 1.2 fusion.34
  286.7 1.4 fusion.6
  288.1 1.5 copy.14
  (3 shorter events, 0.0 us)
Async XLA Ops:
  7.2 71.6 %copy-start = (f32[1,1280,256]{2,1,0:T(8,128)S(1)}, f32[1,1280,256]{2,1,0:T(8,128)}, u32[]{:S(2)}) copy-start(f32[1,1280,256]{2,1,0:T(8,128)} %param.7) | copy-start | bytes 3932164
  7.2 71.6 %reduce-scatter.2.cloned.1.call-start = ((), (), s32[]{:S(2)}) async-start(), calls=%async_computation.1 | async-start | bytes 6963200 | tf_op jit(solution)/shard_map/reduce_scatter | solution.py:45
  7.9 263.6 %all-reduce.2.cloned.1.call-start = ((), (), s32[]{:S(2)}) async-start(), calls=%async_computation.2 | async-start | bytes 2621440 | tf_op jit(solution)/shard_map/psum | solution.py:61
  78.8 1.9 copy-start.2
  80.7 2.3 copy-start.3
  80.7 2.3 copy-start.4
  83.0 0.9 copy-start.5
  271.5 4.4 %copy-start.1 = (f32[1280,256]{0,1:T(8,128)S(1)}, f32[1280,256]{0,1:T(8,128)}, u32[]{:S(2)}) copy-start(f32[1280,256]{0,1:T(8,128)} %all-reduce.2.cloned.1.call-done) | copy-start | bytes 3932164
Sparse Core Ops, SparseCore 0:
  10.5 68.2 reduce-scatter.1
  83.1 188.3 all-reduce.1
where the time goes:
time: 298 us; the launch traced here: 296 us
  waiting for transfers between devices  257 us (86%)
  matrix products  21.4 us (7%)
  between operations  14.9 us (5%)
    psum x1, waiting for transfers between devices, per_device(): power = lax.psum(power_part, ('shard', 'tensor'))  185 us
    reduce_scatter x1, waiting for transfers between devices, per_device(): lax.psum_scatter(gradient, 'shard', scatter_dimension=0, tiled=True)  70.8 us
    dot_general x6, matrix products, inner_rows(): lax.dot_general(left, right, (((0,), (0,)), ((), ())), precision=lax.Prec...  11.2 us
    dot_general x6, matrix products, matmul(): jnp.dot(left, right, precision=lax.Precision.HIGHEST, preferred_element_t...  8.7 us
  transfers between devices with their start and end apart: 2, of which 2 were waited for; matrix products, arithmetic and copies ran while one was open for 1% of the time, Pallas kernels for 0%

commit v1 on v0

--- a/solution.py
+++ b/solution.py
@@ -42,9 +42,15 @@
     gradient = grad_terms[0, 0]
     basis_now = basis[0]
     root_width = math.sqrt(basis_now.shape[0])
-    grad_rows = lax.psum_scatter(gradient, "shard", scatter_dimension=0, tiled=True)
-    low_rank = matmul(grad_rows, basis_now) / root_width
-    power_part = inner_rows(grad_rows, low_rank)
+    rows = first_moment.shape[2]
+    low_rank = lax.psum_scatter(matmul(gradient, basis_now), "shard", scatter_dimension=0, tiled=True) / root_width
+    low_rank_block = lax.all_gather(low_rank, "shard", axis=0, tiled=True)
+    power_part = inner_rows(gradient, low_rank_block)
+    flat = power_part.reshape(-1, 640)
+    power_rows = lax.psum_scatter(flat, "shard", scatter_dimension=0, tiled=True)
+    power_rows = lax.psum_scatter(power_rows, "tensor", scatter_dimension=0, tiled=True)
+    power_rows = lax.all_gather(power_rows, "tensor", axis=0, tiled=True)
+    power = lax.all_gather(power_rows, "shard", axis=0, tiled=True).reshape(power_part.shape)
     moment_one = 0.9 * first_moment[0, 0] + 0.1 * low_rank
     moment_two = 0.95 * second_moment[0, 0] + 0.05 * low_rank * low_rank
     direction = moment_one / (jnp.sqrt(moment_two) + 1e-08)
@@ -58,7 +64,6 @@
     stepped = weights[0, 0].astype(jnp.float32) - 0.5 * update / root_width
     normed = stepped * lax.rsqrt(jnp.mean(stepped * stepped, axis=1, keepdims=True) + 1e-06)
     new_weights = normed.astype(jnp.bfloat16)
-    power = lax.psum(power_part, ("shard", "tensor"))
     iterate = newton_steps(power, local_gram)
     new_basis = iterate * root_width
     return (

time: 298 us -> 318 us (1.067)
  matrix products: 21.4 us -> 37.7 us
  waiting for transfers between devices: 257 us -> 244 us
  blocking collectives: 0 us -> 9.73 us
  local copies, waits for them, and re-layouts: 1.68 us -> 8.53 us
    psum x1 -> x0, waiting for transfers between devices: 185 us -> none  [per_device(): power = lax.psum(power_part, ('shard', 'tensor'))]
    all_gather x0 -> x2, waiting for transfers between devices: none -> 83.8 us  [the longest x1 42.6 us: per_device(): lax.all_gather(power_rows, 'shard', axis=0, tiled=True)]
    unnamed x2 -> x6, waiting for transfers between devices: 0.7 us -> 46.1 us
    reduce_scatter x1 -> x2, waiting for transfers between devices: 70.8 us -> 114 us  [the longest x1 59.8 us: per_device(): lax.psum_scatter(matmul(gradient, basis_now), 'shard', scatter_dimension=...]
    dot_general x6, matrix products: 11.2 us -> 20.9 us  [inner_rows(): lax.dot_general(left, right, (((0,), (0,)), ((), ())), precision=lax.Prec...]
    all_gather x0 -> x1, blocking collectives: none -> 9.73 us  [per_device(): power_rows = lax.all_gather(power_rows, 'tensor', axis=0, tiled=True)]
    dot_general x6, matrix products: 8.7 us -> 15.3 us  [matmul(): jnp.dot(left, right, precision=lax.Precision.HIGHEST, preferred_element_t...]
    reshape x0 -> x2, local copies, waits for them, and re-layouts: none -> 4.47 us  [the longest x1 2.64 us: per_device(): flat = power_part.reshape(-1, 640)]
  transfers between devices with their start and end apart: 2 -> 5, of which waited for: 2 -> 5; matrix products, arithmetic and copies ran while one was open for 1% -> 1% of each run, Pallas kernels for 0% -> 0%
where the time goes in v1:
time: 318 us; the launch traced here: 317 us
  waiting for transfers between devices  244 us (77%)
  matrix products  37.7 us (12%)
  between operations  15.2 us (5%)
  blocking collectives  9.73 us (3%)
  local copies, waits for them, and re-layouts  8.53 us (3%)
    reduce_scatter x1, waiting for transfers between devices, per_device(): lax.psum_scatter(matmul(gradient, basis_now), 'shard', scatter_dimension=...  59.8 us
    reduce_scatter x1, waiting for transfers between devices, per_device(): lax.psum_scatter(flat, 'shard', scatter_dimension=0, tiled=True)  53.9 us
    unnamed x6, waiting for transfers between devices  46.1 us
    all_gather x1, waiting for transfers between devices, per_device(): lax.all_gather(power_rows, 'shard', axis=0, tiled=True)  42.6 us
    all_gather x1, waiting for transfers between devices, per_device(): low_rank_block = lax.all_gather(low_rank, 'shard', axis=0, tiled=True)  41.1 us
    dot_general x6, matrix products, inner_rows(): lax.dot_general(left, right, (((0,), (0,)), ((), ())), precision=lax.Prec...  20.9 us
    dot_general x6, matrix products, matmul(): jnp.dot(left, right, precision=lax.Precision.HIGHEST, preferred_element_t...  15.3 us
    all_gather x1, blocking collectives, per_device(): power_rows = lax.all_gather(power_rows, 'tensor', axis=0, tiled=True)  9.73 us
  transfers between devices with their start and end apart: 5, of which 5 were waited for; matrix products, arithmetic and copies ran while one was open for 1% of the time, Pallas kernels for 0%

profile of v1, /device:TPU:1, one launch (start us, length us, event | category | flops | bytes accessed | tf_op | source)
XLA Modules:
  0.0 317.3 jit_solution(8690136283710917015)
XLA Ops:
  7.2 0.0 reduce-scatter.3.cloned.1.call-start
  7.2 1.3 copy-done
  8.5 8.2 %fusion.2 = f32[1280,256]{1,0:T(8,128)} fusion(f32[1,1,1280,1280]{3,2,1,0:T(8,128)} %param.5, f32[1,1280,256]{2,1,0:T(8,128)S(1)} %copy-done), kind=kOutput, calls=%fused_computation.2 | convolution fusion | flops 5033164800 | bytes 9175040 | tf_op jit(solution)/shard_map/dot_general | solution.py:12
  16.7 0.0 all-gather.3.cloned.1.call-start
  16.8 59.8 %reduce-scatter.3.cloned.1.call-done = f32[80,256]{1,0:T(8,128)} async-done(((f32[1280,256]{1,0:T(8,128)}), f32[80,256]{1,0:T(8,128)}) %reduce-scatter.3.cloned.1.call-update) | async-done | bytes 81936 | tf_op jit(solution)/shard_map/reduce_scatter | solution.py:46
  76.5 1.6 broadcast_multiply_fusion
  78.2 0.0 reduce-scatter.5.cloned.1.call-start
  78.2 41.1 %all-gather.3.cloned.1.call-done = f32[1280,256]{1,0:T(8,128)} async-done(((f32[80,256]{1,0:T(8,128)}), f32[1280,256]{1,0:T(8,128)}) %all-gather.3.cloned.1.call-update) | async-done | bytes 1310736 | tf_op jit(solution)/shard_map/all_gather | solution.py:47
  119.3 8.9 %fusion.11 = f32[1280,256]{0,1:T(8,128)S(1)} fusion(f32[1280,256]{1,0:T(8,128)} %all-gather.3.cloned.1.call-done, f32[1,1,1280,1280]{3,2,1,0:T(8,128)} %param.5), kind=kOutput, calls=%fused_computation.16 | convolution fusion | flops 5033164800 | bytes 9175040 | tf_op jit(solution)/shard_map/dot_general | solution.py:16
  128.2 1.5 copy.10
  129.7 2.6 reshape.28
  132.3 0.0 all-reduce.3.cloned.1.call-start
  132.4 53.9 %reduce-scatter.5.cloned.1.call-done = f32[32,640]{1,0:T(8,128)} async-done(((f32[512,640]{1,0:T(8,128)}), f32[32,640]{1,0:T(8,128)}) %reduce-scatter.5.cloned.1.call-update) | async-done | bytes 81936 | tf_op jit(solution)/shard_map/reduce_scatter | solution.py:50
  186.3 0.0 all-gather.5.cloned.1.call-start
  186.4 0.6 dynamic-slice
  187.6 46.0 %all-reduce.3.cloned.1.call-done = f32[32,640]{1,0:T(8,128)} async-done(((f32[32,640]{1,0:T(8,128)}), f32[32,640]{1,0:T(8,128)}) %all-reduce.3.cloned.1.call-update) | async-done | bytes 81936
  233.6 0.7 constant_dynamic-slice_fusion
  234.3 9.7 %all_gather.10 = f32[32,640]{1,0:T(8,128)} all-gather(f32[8,640]{1,0:T(8,128)S(1)} %constant_dynamic-slice_fusion), channel_id=1, replica_groups=mesh['section'=4,'shard'=16,'tensor'=4] {'tensor'}, dimensions={0}, use_global_device_ids=true | all-gather | bytes 102400 | tf_op jit(solution)/shard_map/all_gather | solution.py:52
  244.1 1.5 multiply_reduce_fusion
  245.6 0.8 fusion.20
  246.4 42.6 %all-gather.5.cloned.1.call-done = f32[512,640]{1,0:T(8,128)} async-done(((f32[32,640]{1,0:T(8,128)}), f32[512,640]{1,0:T(8,128)}) %all-gather.5.cloned.1.call-update) | async-done | bytes 1310736 | tf_op jit(solution)/shard_map/all_gather | solution.py:53
  289.0 1.8 reshape.29
  290.9 2.9 select_reduce_fusion
  294.4 1.2 fusion.9
  295.6 2.2 fusion.34
  297.9 1.2 fusion.8
  299.1 2.2 fusion.35
  301.3 1.2 fusion.7
  302.5 2.5 fusion.36
  305.0 1.2 fusion.6
  306.2 2.2 fusion.37
  308.5 2.3 fusion.10
  (17 shorter events, 0.1 us)
Async XLA Ops:
  7.2 1.3 copy-start
  7.2 69.4 %reduce-scatter.3.cloned.1.call-start = ((), (), s32[]{:S(2)}) async-start(), calls=%async_computation.2 | async-start | bytes 1392640 | tf_op jit(solution)/shard_map/reduce_scatter | solution.py:46
  16.7 59.8 %copy-start.1 = (f32[1,1,80,256]{3,2,1,0:T(8,128)S(1)}, f32[1,1,80,256]{3,2,1,0:T(8,128)}, u32[]{:S(2)}) copy-start(f32[1,1,80,256]{3,2,1,0:T(8,128)} %param.8) | copy-start | bytes 245764
  16.7 59.8 %copy-start.2 = (f32[1,1,80,256]{3,2,1,0:T(8,128)S(1)}, f32[1,1,80,256]{3,2,1,0:T(8,128)}, u32[]{:S(2)}) copy-start(f32[1,1,80,256]{3,2,1,0:T(8,128)} %param.9) | copy-start | bytes 245764
  16.7 102.6 %all-gather.3.cloned.1.call-start = ((), (), s32[]{:S(2)}) async-start(), calls=%async_computation.3 | async-start | bytes 1392640 | tf_op jit(solution)/shard_map/all_gather | solution.py:47
  78.2 108.1 %reduce-scatter.5.cloned.1.call-start = ((), (), s32[]{:S(2)}) async-start(), calls=%async_computation.4 | async-start | bytes 1392640 | tf_op jit(solution)/shard_map/reduce_scatter | solution.py:50
  132.3 54.0 %copy-start.5 = (u32[256]{0:T(256)S(1)}, u32[256]{0:T(256)}, u32[]{:S(2)}) copy-start(u32[256]{0:T(256)} %constant.45) | copy-start | bytes 3076
  132.3 111.8 %copy-start.3 = (f32[80,256]{1,0:T(8,128)S(1)}, f32[80,256]{1,0:T(8,128)}, u32[]{:S(2)}) copy-start(f32[80,256]{1,0:T(8,128)} %reduce-scatter.3.cloned.1.call-done) | copy-start | bytes 245764
  132.3 111.8 %copy-start.4 = (bf16[1,1,80,1280]{3,2,1,0:T(8,128)(2,1)S(1)}, bf16[1,1,80,1280]{3,2,1,0:T(8,128)(2,1)}, u32[]{:S(2)}) copy-start(bf16[1,1,80,1280]{3,2,1,0:T(8,128)(2,1)} %param.6) | copy-start | bytes 614404
  132.3 101.3 %all-reduce.3.cloned.1.call-start = ((), (), s32[]{:S(2)}) async-start(), calls=%async_computation.6 | async-start | bytes 163840
  186.3 102.7 %all-gather.5.cloned.1.call-start = ((), (), s32[]{:S(2)}) async-start(), calls=%async_computation.5 | async-start | bytes 1392640 | tf_op jit(solution)/shard_map/all_gather | solution.py:53
Sparse Core Ops, SparseCore 0:
  16.8 59.6 reduce-scatter.2
  78.9 40.3 all-gather.2
  132.5 53.7 reduce-scatter.4
  188.4 45.1 all-reduce.2
  244.2 44.7 all-gather.4

commit v2 on v0

--- a/solution.py
+++ b/solution.py
@@ -3,7 +3,7 @@
 import jax
 import jax.numpy as jnp
 from jax import lax
-from jax.sharding import PartitionSpec as P
+from jax.sharding import Mesh, PartitionSpec as P
 
 NS_STEPS = 5
 
@@ -38,13 +38,40 @@
     return iterate
 
 
+def swap_cores(x):
+    return lax.ppermute(x, "core", [(0, 1), (1, 0)])
+
+
+def place_halves(own, partner, core):
+    first = jnp.where(core == 0, own, partner)
+    second = jnp.where(core == 0, partner, own)
+    return jnp.stack([first, second])
+
+
 def per_device(grad_terms, weights, basis, first_moment, second_moment):
     gradient = grad_terms[0, 0]
     basis_now = basis[0]
     root_width = math.sqrt(basis_now.shape[0])
-    grad_rows = lax.psum_scatter(gradient, "shard", scatter_dimension=0, tiled=True)
-    low_rank = matmul(grad_rows, basis_now) / root_width
-    power_part = inner_rows(grad_rows, low_rank)
+    rows = first_moment.shape[2]
+    n_z = lax.axis_size("z")
+    core = lax.axis_index("core")
+    partial = matmul(gradient, basis_now).reshape(n_z, 2, rows, -1)
+    own = lax.dynamic_index_in_dim(partial, core, axis=1, keepdims=False)
+    other = lax.dynamic_index_in_dim(partial, 1 - core, axis=1, keepdims=False)
+    chip_sum = own + swap_cores(other)
+    low_rank = lax.all_to_all(chip_sum, "z", 0, 0, tiled=True).sum(axis=0) / root_width
+    gathered = lax.all_to_all(jnp.broadcast_to(low_rank[None], (n_z,) + low_rank.shape), "z", 0, 0, tiled=True)
+    low_rank_block = place_halves(gathered, swap_cores(gathered), core)
+    low_rank_block = jnp.moveaxis(low_rank_block, 0, 1).reshape(gradient.shape[0], -1)
+    power_part = inner_rows(gradient, low_rank_block)
+    n_group = n_z * lax.axis_size("tensor")
+    halves = power_part.reshape(2, n_group, -1, power_part.shape[1])
+    own_half = lax.dynamic_index_in_dim(halves, core, axis=0, keepdims=False)
+    other_half = lax.dynamic_index_in_dim(halves, 1 - core, axis=0, keepdims=False)
+    chip_half = own_half + swap_cores(other_half)
+    piece = lax.all_to_all(chip_half, ("z", "tensor"), 0, 0, tiled=True).sum(axis=0)
+    half = lax.all_to_all(jnp.broadcast_to(piece[None], chip_half.shape), ("z", "tensor"), 0, 0, tiled=True)
+    power = place_halves(half, swap_cores(half), core).reshape(power_part.shape)
     moment_one = 0.9 * first_moment[0, 0] + 0.1 * low_rank
     moment_two = 0.95 * second_moment[0, 0] + 0.05 * low_rank * low_rank
     direction = moment_one / (jnp.sqrt(moment_two) + 1e-08)
@@ -58,7 +85,6 @@
     stepped = weights[0, 0].astype(jnp.float32) - 0.5 * update / root_width
     normed = stepped * lax.rsqrt(jnp.mean(stepped * stepped, axis=1, keepdims=True) + 1e-06)
     new_weights = normed.astype(jnp.bfloat16)
-    power = lax.psum(power_part, ("shard", "tensor"))
     iterate = newton_steps(power, local_gram)
     new_basis = iterate * root_width
     return (
@@ -70,20 +96,23 @@
 
 
 def solution(mesh):
+    devices = mesh.devices.reshape(mesh.shape["section"], -1, 2, mesh.shape["tensor"])
+    split = Mesh(devices, ("section", "z", "core", "tensor"))
+    shard = ("z", "core")
     return jax.shard_map(
         per_device,
-        mesh=mesh,
+        mesh=split,
         in_specs=(
-            P("section", "shard", "tensor", None),
-            P("section", "tensor", "shard", None),
+            P("section", shard, "tensor", None),
+            P("section", "tensor", shard, None),
             P("section", None, None),
-            P("section", "tensor", "shard", None),
-            P("section", "tensor", "shard", None),
+            P("section", "tensor", shard, None),
+            P("section", "tensor", shard, None),
         ),
         out_specs=(
-            P("section", "tensor", "shard", None),
-            P("section", "tensor", "shard", None),
-            P("section", "tensor", "shard", None),
+            P("section", "tensor", shard, None),
+            P("section", "tensor", shard, None),
+            P("section", "tensor", shard, None),
             P("section", None, None),
         ),
         check_vma=False,

time: 298 us -> 167 us (0.56)
  waiting for transfers between devices: 257 us -> 25.3 us
  blocking collectives: 0 us -> 72.1 us
  matrix products: 21.4 us -> 38.9 us
  starting transfers between devices: 0.08 us -> 15.9 us
  between operations: 14.9 us -> 1.61 us
  local copies, waits for them, and re-layouts: 1.68 us -> 10.3 us
    psum x1 -> x0, waiting for transfers between devices: 185 us -> none  [per_device(): power = lax.psum(power_part, ('shard', 'tensor'))]
    all_to_all x0 -> x3, blocking collectives: none -> 72.1 us  [the longest x1 25.8 us: per_device(): lax.all_to_all(chip_sum, 'z', 0, 0, tiled=True).sum(axis=0) / root_width]
    reduce_scatter x1 -> x0, waiting for transfers between devices: 70.8 us -> none  [per_device(): lax.psum_scatter(gradient, 'shard', scatter_dimension=0, tiled=True)]
    all_to_all x0 -> x1, waiting for transfers between devices: none -> 19 us  [per_device(): lax.all_to_all(jnp.broadcast_to(piece[None], chip_half.shape), ('z', 'ten...]
    ppermute x0 -> x4, starting transfers between devices: none -> 10.1 us  [swap_cores(): return lax.ppermute(x, 'core', [(0, 1), (1, 0)])]
    dot_general x6, matrix products: 11.2 us -> 21.2 us  [inner_rows(): lax.dot_general(left, right, (((0,), (0,)), ((), ())), precision=lax.Prec...]
    dot_general x6, matrix products: 8.7 us -> 16.2 us  [matmul(): jnp.dot(left, right, precision=lax.Precision.HIGHEST, preferred_element_t...]
    ppermute x0 -> x4, waiting for transfers between devices: none -> 6.32 us  [swap_cores(): return lax.ppermute(x, 'core', [(0, 1), (1, 0)])]
  transfers between devices with their start and end apart: 2 -> 5, of which waited for: 2 -> 5; matrix products, arithmetic and copies ran while one was open for 1% -> 1% of each run, Pallas kernels for 0% -> 0%
where the time goes in v2:
time: 167 us
  blocking collectives  72.1 us (43%)
  matrix products  38.9 us (23%)
  waiting for transfers between devices  25.3 us (15%)
  starting transfers between devices  15.9 us (10%)
  local copies, waits for them, and re-layouts  10.3 us (6%)
  other arithmetic  2.91 us (2%)
    all_to_all x1, blocking collectives, per_device(): lax.all_to_all(chip_sum, 'z', 0, 0, tiled=True).sum(axis=0) / root_width  25.8 us
    all_to_all x1, blocking collectives, per_device(): lax.all_to_all(chip_half, ('z', 'tensor'), 0, 0, tiled=True).sum(axis=0)  25.7 us
    dot_general x6, matrix products, inner_rows(): lax.dot_general(left, right, (((0,), (0,)), ((), ())), precision=lax.Prec...  21.2 us
    all_to_all x1, blocking collectives, per_device(): lax.all_to_all(jnp.broadcast_to(low_rank[None], (n_z,) + low_rank.shape),...  20.6 us
    all_to_all x1, waiting for transfers between devices, per_device(): lax.all_to_all(jnp.broadcast_to(piece[None], chip_half.shape), ('z', 'ten...  19 us
    dot_general x6, matrix products, matmul(): jnp.dot(left, right, precision=lax.Precision.HIGHEST, preferred_element_t...  16.2 us
    ppermute x4, starting transfers between devices, swap_cores(): return lax.ppermute(x, 'core', [(0, 1), (1, 0)])  10.1 us
    ppermute x4, waiting for transfers between devices, swap_cores(): return lax.ppermute(x, 'core', [(0, 1), (1, 0)])  6.32 us
  transfers between devices with their start and end apart: 5, of which 5 were waited for; matrix products, arithmetic and copies ran while one was open for 1% of the time, Pallas kernels for 0%

profile of v2, /device:TPU:1, one launch (start us, length us, event | category | flops | bytes accessed | tf_op | source)
XLA Modules:
  0.0 167.0 jit_solution(12952986789419554718)
XLA Ops:
  0.7 1.3 copy-done
  2.0 7.4 %fusion.13 = f32[8,2,80,256]{3,2,1,0:T(8,128)S(1)} fusion(f32[8,2,80,1280]{3,2,1,0:T(8,128)} %bitcast.80, f32[1,1280,256]{2,1,0:T(8,128)S(1)} %copy-done), kind=kOutput, calls=%fused_computation.19 | convolution fusion | flops 5033164800 | bytes 9175040 | tf_op jit(solution)/shard_map/dot_general | solution.py:12
  10.3 3.2 %collective-permute-start = (f32[8,80,256]{2,1,0:T(8,128)}, f32[8,80,256]{2,1,0:T(8,128)S(1)}, u32[]{:S(2)}, u32[]{:S(2)}) collective-permute-start(f32[8,80,256]{2,1,0:T(8,128)} %dynamic-slice_bitcast_fusion), channel_id=1, source_target_pairs={{0,4},{4,0},{1,5},{5,1},{2,6},{6,2},{3,7},{7,3},{8,12},{12,8},{9,1... | collective-permute-start | bytes 1966088 | tf_op jit(solution)/shard_map/ppermute | solution.py:42
  13.5 1.9 %collective-permute-done = f32[8,80,256]{2,1,0:T(8,128)S(1)} collective-permute-done((f32[8,80,256]{2,1,0:T(8,128)}, f32[8,80,256]{2,1,0:T(8,128)S(1)}, u32[]{:S(2)}, u32[]{:S(2)}) %collective-permute-start) | collective-permute-done | bytes 655392 | tf_op jit(solution)/shard_map/ppermute | solution.py:42
  15.5 25.8 %all_to_all.20 = f32[8,80,256]{2,1,0:T(8,128)S(1)} all-to-all(f32[8,80,256]{2,1,0:T(8,128)S(1)} %bitcast_add_fusion.1), channel_id=1, replica_groups=mesh['section'=4,'z'=8,'core'=2,'tensor'=4] {'z'}, dimensions={0} | all-to-all | bytes 1310720 | tf_op jit(solution)/shard_map/all_to_all | solution.py:62
  41.4 20.6 %all_to_all.21 = f32[8,80,256]{2,1,0:T(8,128)S(1)} all-to-all(f32[8,80,256]{2,1,0:T(8,128)S(1)} %broadcast_in_dim.13), channel_id=1, replica_groups=mesh['section'=4,'z'=8,'core'=2,'tensor'=4] {'z'}, dimensions={0} | all-to-all | bytes 1310720 | tf_op jit(solution)/shard_map/all_to_all | solution.py:63
  62.0 3.0 %collective-permute-start.1 = (f32[8,80,256]{2,1,0:T(8,128)S(1)}, f32[8,80,256]{2,1,0:T(8,128)S(1)}, u32[]{:S(2)}, u32[]{:S(2)}) collective-permute-start(f32[8,80,256]{2,1,0:T(8,128)S(1)} %all_to_all.21), channel_id=1, source_target_pairs={{0,4},{4,0},{1,5},{5,1},{2,6},{6,2},{3,7},{7,3},{8,12},{12,8},{9,1... | collective-permute-start | bytes 1966088 | tf_op jit(solution)/shard_map/ppermute | solution.py:42
  65.1 1.7 %collective-permute-done.1 = f32[8,80,256]{2,1,0:T(8,128)S(1)} collective-permute-done((f32[8,80,256]{2,1,0:T(8,128)S(1)}, f32[8,80,256]{2,1,0:T(8,128)S(1)}, u32[]{:S(2)}, u32[]{:S(2)}) %collective-permute-start.1) | collective-permute-done | bytes 655392 | tf_op jit(solution)/shard_map/ppermute | solution.py:42
  67.0 8.5 %fusion.9 = f32[1280,256]{0,1:T(8,128)S(1)} fusion(f32[1280,256]{1,0:T(8,128)S(1)} %bitcast.81, f32[1,1,1280,1280]{3,2,1,0:T(8,128)} %param.5), kind=kOutput, calls=%fused_computation.14 | convolution fusion | flops 5033164800 | bytes 9175040 | tf_op jit(solution)/shard_map/dot_general | solution.py:16
  75.5 1.5 copy.27
  77.0 1.4 reshape.64
  79.4 1.7 %collective-permute-done.2 = f32[32,20,256]{2,0,1:T(8,128)S(1)} collective-permute-done((f32[32,20,256]{2,0,1:T(8,128)S(1)}, f32[32,20,256]{2,0,1:T(8,128)S(1)}, u32[]{:S(2)}, u32[]{:S(2)}) %collective-permute-start.2) | collective-permute-done | bytes 655392 | tf_op jit(solution)/shard_map/ppermute | solution.py:42
  81.7 25.7 %all_to_all.22 = f32[32,20,256]{2,1,0:T(8,128)S(1)} all-to-all(f32[32,20,256]{2,1,0:T(8,128)S(1)} %copy.30), channel_id=1, replica_groups=mesh['section'=4,'z'=8,'core'=2,'tensor'=4] {'z','tensor'}, dimensions={0} | all-to-all | bytes 1310720 | tf_op jit(solution)/shard_map/all_to_all | solution.py:72
  107.5 0.9 broadcast_in_dim.14
  108.4 5.8 %all-to-all-start.3 = ((f32[32,20,256]{2,1,0:T(8,128)}), f32[32,20,256]{2,1,0:T(8,128)S(1)}, u32[]{:S(2)}, u32[]{:S(2)}) async-start(f32[32,20,256]{2,1,0:T(8,128)} %broadcast_in_dim.14), calls=%async_computation.3 | async-start | bytes 1572864 | tf_op jit(solution)/shard_map/all_to_all | solution.py:73
  114.4 1.5 multiply_reduce_fusion
  115.8 19.0 %all-to-all-done.3 = f32[32,20,256]{2,1,0:T(8,128)S(1)} async-done(((f32[32,20,256]{2,1,0:T(8,128)}), f32[32,20,256]{2,1,0:T(8,128)S(1)}, u32[]{:S(2)}, u32[]{:S(2)}) %all-to-all-start.3) | async-done | bytes 655392 | tf_op jit(solution)/shard_map/all_to_all | solution.py:73
  135.0 3.2 %collective-permute-start.3 = (f32[32,20,256]{2,0,1:T(8,128)S(1)}, f32[32,20,256]{2,0,1:T(8,128)S(1)}, u32[]{:S(2)}, u32[]{:S(2)}) collective-permute-start(f32[32,20,256]{2,0,1:T(8,128)S(1)} %copy.32), channel_id=1, source_target_pairs={{0,4},{4,0},{1,5},{5,1},{2,6},{6,2},{3,7},{7,3},{8,12},{12,8},{9,1... | collective-permute-start | bytes 1966088 | tf_op jit(solution)/shard_map/ppermute | solution.py:42
  139.0 0.9 collective-permute-done.3
  140.2 3.5 %select_reduce_fusion = (f32[]{:T(128)}, f32[256,256]{1,0:T(8,128)}) fusion(f32[1,32,20,256]{3,1,2,0:T(8,128)S(1)} %get-tuple-element.7, f32[1,32,20,256]{3,1,2,0:T(8,128)S(1)} %get-tuple-element.6), kind=kOutput, calls=%fused_computation.35 | convolution fusion | flops 1007157248 | bytes 1572868 | tf_op jit(solution)/shard_map/dot_general | solution.py:16
  144.5 1.2 fusion.16
  145.6 2.1 %copy.34 = f32[2,32,20,256]{3,2,1,0:T(8,128)S(1)} copy(f32[2,32,20,256]{3,1,2,0:T(8,128)} %fusion.16) | data formatting | bytes 2621440 | tf_op jit(solution)/shard_map/mul | solution.py:32
  147.7 1.2 mul.145
  148.9 3.0 %fusion.7 = f32[1280,256]{1,0:T(8,128)S(1)} fusion(f32[1280,256]{1,0:T(8,128)} %mul.145, f32[256,256]{1,0:T(8,128)S(1)} %copy-done.3, f32[]{:T(128)S(6)} %mul.147), kind=kOutput, calls=%fused_computation.12 | convolution fusion | flops 1007681536 | bytes 2883588 | tf_op jit(solution)/shard_map/dot_general | solution.py:12
  151.9 2.2 %fusion.27 = f32[256,256]{1,0:T(8,128)S(1)} fusion(f32[1280,256]{1,0:T(8,128)S(1)} %fusion.7), kind=kOutput, calls=%fused_computation.52 | convolution fusion | flops 1006632960 | bytes 1572864 | tf_op jit(solution)/shard_map/dot_general | solution.py:16
  154.1 1.2 fusion.6
  155.3 2.2 %fusion.28 = f32[256,256]{1,0:T(8,128)S(1)} fusion(f32[1280,256]{1,0:T(8,128)S(1)} %fusion.6), kind=kOutput, calls=%fused_computation.53 | convolution fusion | flops 1006632960 | bytes 1572864 | tf_op jit(solution)/shard_map/dot_general | solution.py:16
  157.6 1.2 fusion.5
  158.8 2.5 %fusion.29 = f32[256,256]{1,0:T(8,128)S(1)} fusion(f32[1280,256]{1,0:T(8,128)S(1)} %fusion.5), kind=kOutput, calls=%fused_computation.54 | convolution fusion | flops 1006632960 | bytes 1572864 | tf_op jit(solution)/shard_map/dot_general | solution.py:16
  161.3 1.2 fusion.4
  162.5 2.2 %fusion.30 = f32[256,256]{1,0:T(8,128)S(1)} fusion(f32[1280,256]{1,0:T(8,128)S(1)} %fusion.4), kind=kOutput, calls=%fused_computation.55 | convolution fusion | flops 1006632960 | bytes 1572864 | tf_op jit(solution)/shard_map/dot_general | solution.py:16
  164.7 2.3 %fusion.8 = f32[1,1280,256]{2,1,0:T(8,128)} fusion(f32[1280,256]{1,0:T(8,128)S(1)} %fusion.4, f32[256,256]{1,0:T(8,128)S(1)} %fusion.30), kind=kOutput, calls=%fused_computation.13 | convolution fusion | flops 1007943680 | bytes 2883584 | tf_op jit(solution)/shard_map/dot_general | solution.py:12
  (31 shorter events, 4.3 us)
Async XLA Ops:
  0.6 1.3 copy-start
  10.3 5.1 %collective-permute-start = (f32[8,80,256]{2,1,0:T(8,128)}, f32[8,80,256]{2,1,0:T(8,128)S(1)}, u32[]{:S(2)}, u32[]{:S(2)}) collective-permute-start(f32[8,80,256]{2,1,0:T(8,128)} %dynamic-slice_bitcast_fusion), channel_id=1, source_target_pairs={{0,4},{4,0},{1,5},{5,1},{2,6},{6,2},{3,7},{7,3},{8,12},{12,8},{9,1... | collective-permute-start | bytes 1966088 | tf_op jit(solution)/shard_map/ppermute | solution.py:42
  62.0 4.8 %collective-permute-start.1 = (f32[8,80,256]{2,1,0:T(8,128)S(1)}, f32[8,80,256]{2,1,0:T(8,128)S(1)}, u32[]{:S(2)}, u32[]{:S(2)}) collective-permute-start(f32[8,80,256]{2,1,0:T(8,128)S(1)} %all_to_all.21), channel_id=1, source_target_pairs={{0,4},{4,0},{1,5},{5,1},{2,6},{6,2},{3,7},{7,3},{8,12},{12,8},{9,1... | collective-permute-start | bytes 1966088 | tf_op jit(solution)/shard_map/ppermute | solution.py:42
  78.7 2.4 %collective-permute-start.2 = (f32[32,20,256]{2,0,1:T(8,128)S(1)}, f32[32,20,256]{2,0,1:T(8,128)S(1)}, u32[]{:S(2)}, u32[]{:S(2)}) collective-permute-start(f32[32,20,256]{2,0,1:T(8,128)S(1)} %bitcast.82), channel_id=1, source_target_pairs={{0,4},{4,0},{1,5},{5,1},{2,6},{6,2},{3,7},{7,3},{8,12},{12,8},{9,1... | collective-permute-start | bytes 1966088 | tf_op jit(solution)/shard_map/ppermute | solution.py:42
  107.5 6.8 %copy-start.5 = (f32[1,1,80,256]{3,2,1,0:T(8,128)S(1)}, f32[1,1,80,256]{3,2,1,0:T(8,128)}, u32[]{:S(2)}) copy-start(f32[1,1,80,256]{3,2,1,0:T(8,128)} %param.9) | copy-start | bytes 245764
  107.5 6.8 %copy-start.6 = (f32[1,1,80,256]{3,2,1,0:T(8,128)S(1)}, f32[1,1,80,256]{3,2,1,0:T(8,128)}, u32[]{:S(2)}) copy-start(f32[1,1,80,256]{3,2,1,0:T(8,128)} %param.8) | copy-start | bytes 245764
  107.5 6.9 %copy-start.4 = (bf16[1,1,80,1280]{3,2,1,0:T(8,128)(2,1)S(1)}, bf16[1,1,80,1280]{3,2,1,0:T(8,128)(2,1)}, u32[]{:S(2)}) copy-start(bf16[1,1,80,1280]{3,2,1,0:T(8,128)(2,1)} %param.6) | copy-start | bytes 614404
  108.4 26.4 %all-to-all-start.3 = ((f32[32,20,256]{2,1,0:T(8,128)}), f32[32,20,256]{2,1,0:T(8,128)S(1)}, u32[]{:S(2)}, u32[]{:S(2)}) async-start(f32[32,20,256]{2,1,0:T(8,128)} %broadcast_in_dim.14), calls=%async_computation.3 | async-start | bytes 1572864 | tf_op jit(solution)/shard_map/all_to_all | solution.py:73
  114.3 20.7 %copy-start.1 = (f32[1,1,80,256]{3,2,1,0:T(8,128)}, f32[1,1,80,256]{3,2,1,0:T(8,128)S(1)}, u32[]{:S(2)}) copy-start(f32[1,1,80,256]{3,2,1,0:T(8,128)S(1)} %get-tuple-element.10) | copy-start | bytes 245764
  114.3 20.7 %copy-start.2 = (f32[1,1,80,256]{3,2,1,0:T(8,128)}, f32[1,1,80,256]{3,2,1,0:T(8,128)S(1)}, u32[]{:S(2)}) copy-start(f32[1,1,80,256]{3,2,1,0:T(8,128)S(1)} %get-tuple-element.11) | copy-start | bytes 245764
  135.0 4.9 %collective-permute-start.3 = (f32[32,20,256]{2,0,1:T(8,128)S(1)}, f32[32,20,256]{2,0,1:T(8,128)S(1)}, u32[]{:S(2)}, u32[]{:S(2)}) collective-permute-start(f32[32,20,256]{2,0,1:T(8,128)S(1)} %copy.32), channel_id=1, source_target_pairs={{0,4},{4,0},{1,5},{5,1},{2,6},{6,2},{3,7},{7,3},{8,12},{12,8},{9,1... | collective-permute-start | bytes 1966088 | tf_op jit(solution)/shard_map/ppermute | solution.py:42
  147.7 1.2 copy-start.3

commit v3 on v2

--- a/solution.py
+++ b/solution.py
@@ -9,7 +9,7 @@
 
 
 def matmul(left, right):
-    return jnp.dot(left, right, precision=lax.Precision.HIGHEST, preferred_element_type=jnp.float32)
+    return jnp.dot(left, right, precision=lax.Precision.HIGH, preferred_element_type=jnp.float32)
 
 
 def inner_rows(left, right):
@@ -17,7 +17,7 @@
         left,
         right,
         (((0,), (0,)), ((), ())),
-        precision=lax.Precision.HIGHEST,
+        precision=lax.Precision.HIGH,
         preferred_element_type=jnp.float32,
     )
 
@@ -79,7 +79,7 @@
         direction,
         basis_now,
         (((1,), (1,)), ((), ())),
-        precision=lax.Precision.HIGHEST,
+        precision=lax.Precision.HIGH,
         preferred_element_type=jnp.float32,
     )
     stepped = weights[0, 0].astype(jnp.float32) - 0.5 * update / root_width

time: 167 us -> 154 us (0.922)
  matrix products: 38.9 us -> 25.1 us
    dot_general x6, matrix products: 21.2 us -> 13.1 us  [inner_rows(): lax.dot_general(left, right, (((0,), (0,)), ((), ())), precision=lax.Prec...]
    dot_general x6, matrix products: 16.2 us -> 11.1 us  [matmul(): jnp.dot(left, right, precision=lax.Precision.HIGH, preferred_element_type...]
where the time goes in v3:
time: 154 us
  blocking collectives  72.1 us (47%)
  waiting for transfers between devices  25.9 us (17%)
  matrix products  25.1 us (16%)
  starting transfers between devices  15.9 us (10%)
  local copies, waits for them, and re-layouts  10.3 us (7%)
  other arithmetic  2.91 us (2%)
  between operations  1.61 us (1%)
    all_to_all x1, blocking collectives, per_device(): lax.all_to_all(chip_sum, 'z', 0, 0, tiled=True).sum(axis=0) / root_width  25.8 us
    all_to_all x1, blocking collectives, per_device(): lax.all_to_all(chip_half, ('z', 'tensor'), 0, 0, tiled=True).sum(axis=0)  25.7 us
    all_to_all x1, blocking collectives, per_device(): lax.all_to_all(jnp.broadcast_to(low_rank[None], (n_z,) + low_rank.shape),...  20.6 us
    all_to_all x1, waiting for transfers between devices, per_device(): lax.all_to_all(jnp.broadcast_to(piece[None], chip_half.shape), ('z', 'ten...  19.6 us
    dot_general x6, matrix products, inner_rows(): lax.dot_general(left, right, (((0,), (0,)), ((), ())), precision=lax.Prec...  13.1 us
    dot_general x6, matrix products, matmul(): jnp.dot(left, right, precision=lax.Precision.HIGH, preferred_element_type...  11.1 us
    ppermute x4, starting transfers between devices, swap_cores(): return lax.ppermute(x, 'core', [(0, 1), (1, 0)])  10.1 us
    ppermute x4, waiting for transfers between devices, swap_cores(): return lax.ppermute(x, 'core', [(0, 1), (1, 0)])  6.32 us
  transfers between devices with their start and end apart: 5, of which 5 were waited for; matrix products, arithmetic and copies ran while one was open for 1% of the time, Pallas kernels for 0%

profile of v3, /device:TPU:1, one launch (start us, length us, event | category | flops | bytes accessed | tf_op | source)
XLA Modules:
  0.0 153.8 jit_solution(3093506627618887132)
XLA Ops:
  0.7 1.3 copy-done
  2.0 4.9 %fusion.13 = f32[8,2,80,256]{3,2,1,0:T(8,128)S(1)} fusion(f32[8,2,80,1280]{3,2,1,0:T(8,128)} %bitcast.80, f32[1,1280,256]{2,1,0:T(8,128)S(1)} %copy-done), kind=kOutput, calls=%fused_computation.19 | convolution fusion | flops 2516582400 | bytes 9175040 | tf_op jit(solution)/shard_map/dot_general | solution.py:12
  6.8 0.9 dynamic-slice_bitcast_fusion
  7.8 3.2 %collective-permute-start = (f32[8,80,256]{2,1,0:T(8,128)}, f32[8,80,256]{2,1,0:T(8,128)S(1)}, u32[]{:S(2)}, u32[]{:S(2)}) collective-permute-start(f32[8,80,256]{2,1,0:T(8,128)} %dynamic-slice_bitcast_fusion), channel_id=1, source_target_pairs={{0,4},{4,0},{1,5},{5,1},{2,6},{6,2},{3,7},{7,3},{8,12},{12,8},{9,1... | collective-permute-start | bytes 1966088 | tf_op jit(solution)/shard_map/ppermute | solution.py:42
  11.0 1.9 %collective-permute-done = f32[8,80,256]{2,1,0:T(8,128)S(1)} collective-permute-done((f32[8,80,256]{2,1,0:T(8,128)}, f32[8,80,256]{2,1,0:T(8,128)S(1)}, u32[]{:S(2)}, u32[]{:S(2)}) %collective-permute-start) | collective-permute-done | bytes 655392 | tf_op jit(solution)/shard_map/ppermute | solution.py:42
  13.0 25.8 %all_to_all.20 = f32[8,80,256]{2,1,0:T(8,128)S(1)} all-to-all(f32[8,80,256]{2,1,0:T(8,128)S(1)} %bitcast_add_fusion.1), channel_id=1, replica_groups=mesh['section'=4,'z'=8,'core'=2,'tensor'=4] {'z'}, dimensions={0} | all-to-all | bytes 1310720 | tf_op jit(solution)/shard_map/all_to_all | solution.py:62
  38.9 20.6 %all_to_all.21 = f32[8,80,256]{2,1,0:T(8,128)S(1)} all-to-all(f32[8,80,256]{2,1,0:T(8,128)S(1)} %broadcast_in_dim.13), channel_id=1, replica_groups=mesh['section'=4,'z'=8,'core'=2,'tensor'=4] {'z'}, dimensions={0} | all-to-all | bytes 1310720 | tf_op jit(solution)/shard_map/all_to_all | solution.py:63
  59.5 3.0 %collective-permute-start.1 = (f32[8,80,256]{2,1,0:T(8,128)S(1)}, f32[8,80,256]{2,1,0:T(8,128)S(1)}, u32[]{:S(2)}, u32[]{:S(2)}) collective-permute-start(f32[8,80,256]{2,1,0:T(8,128)S(1)} %all_to_all.21), channel_id=1, source_target_pairs={{0,4},{4,0},{1,5},{5,1},{2,6},{6,2},{3,7},{7,3},{8,12},{12,8},{9,1... | collective-permute-start | bytes 1966088 | tf_op jit(solution)/shard_map/ppermute | solution.py:42
  62.6 1.7 %collective-permute-done.1 = f32[8,80,256]{2,1,0:T(8,128)S(1)} collective-permute-done((f32[8,80,256]{2,1,0:T(8,128)S(1)}, f32[8,80,256]{2,1,0:T(8,128)S(1)}, u32[]{:S(2)}, u32[]{:S(2)}) %collective-permute-start.1) | collective-permute-done | bytes 655392 | tf_op jit(solution)/shard_map/ppermute | solution.py:42
  64.5 5.8 %fusion.9 = f32[1280,256]{0,1:T(8,128)S(1)} fusion(f32[1280,256]{1,0:T(8,128)S(1)} %bitcast.81, f32[1,1,1280,1280]{3,2,1,0:T(8,128)} %param.5), kind=kOutput, calls=%fused_computation.14 | convolution fusion | flops 2516582400 | bytes 9175040 | tf_op jit(solution)/shard_map/dot_general | solution.py:16
  70.3 1.5 copy.27
  71.8 1.4 reshape.64
  74.0 1.7 %collective-permute-done.2 = f32[32,20,256]{2,0,1:T(8,128)S(1)} collective-permute-done((f32[32,20,256]{2,0,1:T(8,128)S(1)}, f32[32,20,256]{2,0,1:T(8,128)S(1)}, u32[]{:S(2)}, u32[]{:S(2)}) %collective-permute-start.2) | collective-permute-done | bytes 655392 | tf_op jit(solution)/shard_map/ppermute | solution.py:42
  76.4 25.7 %all_to_all.22 = f32[32,20,256]{2,1,0:T(8,128)S(1)} all-to-all(f32[32,20,256]{2,1,0:T(8,128)S(1)} %copy.30), channel_id=1, replica_groups=mesh['section'=4,'z'=8,'core'=2,'tensor'=4] {'z','tensor'}, dimensions={0} | all-to-all | bytes 1310720 | tf_op jit(solution)/shard_map/all_to_all | solution.py:72
  102.1 0.9 broadcast_in_dim.14
  103.1 5.8 %all-to-all-start.3 = ((f32[32,20,256]{2,1,0:T(8,128)}), f32[32,20,256]{2,1,0:T(8,128)S(1)}, u32[]{:S(2)}, u32[]{:S(2)}) async-start(f32[32,20,256]{2,1,0:T(8,128)} %broadcast_in_dim.14), calls=%async_computation.3 | async-start | bytes 1572864 | tf_op jit(solution)/shard_map/all_to_all | solution.py:73
  109.0 0.8 multiply_reduce_fusion
  109.8 19.6 %all-to-all-done.3 = f32[32,20,256]{2,1,0:T(8,128)S(1)} async-done(((f32[32,20,256]{2,1,0:T(8,128)}), f32[32,20,256]{2,1,0:T(8,128)S(1)}, u32[]{:S(2)}, u32[]{:S(2)}) %all-to-all-start.3) | async-done | bytes 655392 | tf_op jit(solution)/shard_map/all_to_all | solution.py:73
  129.7 3.4 %collective-permute-start.3 = (f32[32,20,256]{2,0,1:T(8,128)S(1)}, f32[32,20,256]{2,0,1:T(8,128)S(1)}, u32[]{:S(2)}, u32[]{:S(2)}) collective-permute-start(f32[32,20,256]{2,0,1:T(8,128)S(1)} %copy.32), channel_id=1, source_target_pairs={{0,4},{4,0},{1,5},{5,1},{2,6},{6,2},{3,7},{7,3},{8,12},{12,8},{9,1... | collective-permute-start | bytes 1966088 | tf_op jit(solution)/shard_map/ppermute | solution.py:42
  133.0 0.8 fusion.18
  133.8 0.9 collective-permute-done.3
  135.0 2.5 %select_reduce_fusion = (f32[]{:T(128)}, f32[256,256]{1,0:T(8,128)}) fusion(f32[1,32,20,256]{3,1,2,0:T(8,128)S(1)} %get-tuple-element.7, f32[1,32,20,256]{3,1,2,0:T(8,128)S(1)} %get-tuple-element.6), kind=kOutput, calls=%fused_computation.35 | convolution fusion | flops 503840768 | bytes 1572868 | tf_op jit(solution)/shard_map/dot_general | solution.py:16
  138.2 1.2 fusion.16
  139.4 2.1 %copy.34 = f32[2,32,20,256]{3,2,1,0:T(8,128)S(1)} copy(f32[2,32,20,256]{3,1,2,0:T(8,128)} %fusion.16) | data formatting | bytes 2621440 | tf_op jit(solution)/shard_map/mul | solution.py:32
  141.5 1.2 mul.145
  142.7 2.5 %fusion.7 = f32[1280,256]{1,0:T(8,128)S(1)} fusion(f32[1280,256]{1,0:T(8,128)} %mul.145, f32[256,256]{1,0:T(8,128)S(1)} %copy-done.3, f32[]{:T(128)S(6)} %mul.147), kind=kOutput, calls=%fused_computation.12 | convolution fusion | flops 504365056 | bytes 2883588 | tf_op jit(solution)/shard_map/dot_general | solution.py:12
  145.1 1.2 fusion.27
  147.0 1.2 fusion.28
  148.9 1.2 fusion.29
  150.2 0.7 fusion.4
  150.8 1.2 fusion.30
  152.1 1.7 %fusion.8 = f32[1,1280,256]{2,1,0:T(8,128)} fusion(f32[1280,256]{1,0:T(8,128)S(1)} %fusion.4, f32[256,256]{1,0:T(8,128)S(1)} %fusion.30), kind=kOutput, calls=%fused_computation.13 | convolution fusion | flops 504627200 | bytes 2883584 | tf_op jit(solution)/shard_map/dot_general | solution.py:12
  (31 shorter events, 3.8 us)
Async XLA Ops:
  0.6 1.3 copy-start
  7.8 5.1 %collective-permute-start = (f32[8,80,256]{2,1,0:T(8,128)}, f32[8,80,256]{2,1,0:T(8,128)S(1)}, u32[]{:S(2)}, u32[]{:S(2)}) collective-permute-start(f32[8,80,256]{2,1,0:T(8,128)} %dynamic-slice_bitcast_fusion), channel_id=1, source_target_pairs={{0,4},{4,0},{1,5},{5,1},{2,6},{6,2},{3,7},{7,3},{8,12},{12,8},{9,1... | collective-permute-start | bytes 1966088 | tf_op jit(solution)/shard_map/ppermute | solution.py:42
  59.5 4.8 %collective-permute-start.1 = (f32[8,80,256]{2,1,0:T(8,128)S(1)}, f32[8,80,256]{2,1,0:T(8,128)S(1)}, u32[]{:S(2)}, u32[]{:S(2)}) collective-permute-start(f32[8,80,256]{2,1,0:T(8,128)S(1)} %all_to_all.21), channel_id=1, source_target_pairs={{0,4},{4,0},{1,5},{5,1},{2,6},{6,2},{3,7},{7,3},{8,12},{12,8},{9,1... | collective-permute-start | bytes 1966088 | tf_op jit(solution)/shard_map/ppermute | solution.py:42
  73.5 2.2 %collective-permute-start.2 = (f32[32,20,256]{2,0,1:T(8,128)S(1)}, f32[32,20,256]{2,0,1:T(8,128)S(1)}, u32[]{:S(2)}, u32[]{:S(2)}) collective-permute-start(f32[32,20,256]{2,0,1:T(8,128)S(1)} %bitcast.82), channel_id=1, source_target_pairs={{0,4},{4,0},{1,5},{5,1},{2,6},{6,2},{3,7},{7,3},{8,12},{12,8},{9,1... | collective-permute-start | bytes 1966088 | tf_op jit(solution)/shard_map/ppermute | solution.py:42
  102.1 6.8 %copy-start.5 = (f32[1,1,80,256]{3,2,1,0:T(8,128)S(1)}, f32[1,1,80,256]{3,2,1,0:T(8,128)}, u32[]{:S(2)}) copy-start(f32[1,1,80,256]{3,2,1,0:T(8,128)} %param.9) | copy-start | bytes 245764
  102.1 6.8 %copy-start.6 = (f32[1,1,80,256]{3,2,1,0:T(8,128)S(1)}, f32[1,1,80,256]{3,2,1,0:T(8,128)}, u32[]{:S(2)}) copy-start(f32[1,1,80,256]{3,2,1,0:T(8,128)} %param.8) | copy-start | bytes 245764
  102.1 6.9 %copy-start.4 = (bf16[1,1,80,1280]{3,2,1,0:T(8,128)(2,1)S(1)}, bf16[1,1,80,1280]{3,2,1,0:T(8,128)(2,1)}, u32[]{:S(2)}) copy-start(bf16[1,1,80,1280]{3,2,1,0:T(8,128)(2,1)} %param.6) | copy-start | bytes 614404
  103.1 26.4 %all-to-all-start.3 = ((f32[32,20,256]{2,1,0:T(8,128)}), f32[32,20,256]{2,1,0:T(8,128)S(1)}, u32[]{:S(2)}, u32[]{:S(2)}) async-start(f32[32,20,256]{2,1,0:T(8,128)} %broadcast_in_dim.14), calls=%async_computation.3 | async-start | bytes 1572864 | tf_op jit(solution)/shard_map/all_to_all | solution.py:73
  109.0 20.7 %copy-start.1 = (f32[1,1,80,256]{3,2,1,0:T(8,128)}, f32[1,1,80,256]{3,2,1,0:T(8,128)S(1)}, u32[]{:S(2)}) copy-start(f32[1,1,80,256]{3,2,1,0:T(8,128)S(1)} %get-tuple-element.10) | copy-start | bytes 245764
  109.0 20.7 %copy-start.2 = (f32[1,1,80,256]{3,2,1,0:T(8,128)}, f32[1,1,80,256]{3,2,1,0:T(8,128)S(1)}, u32[]{:S(2)}) copy-start(f32[1,1,80,256]{3,2,1,0:T(8,128)S(1)} %get-tuple-element.11) | copy-start | bytes 245764
  129.7 5.1 %collective-permute-start.3 = (f32[32,20,256]{2,0,1:T(8,128)S(1)}, f32[32,20,256]{2,0,1:T(8,128)S(1)}, u32[]{:S(2)}, u32[]{:S(2)}) collective-permute-start(f32[32,20,256]{2,0,1:T(8,128)S(1)} %copy.32), channel_id=1, source_target_pairs={{0,4},{4,0},{1,5},{5,1},{2,6},{6,2},{3,7},{7,3},{8,12},{12,8},{9,1... | collective-permute-start | bytes 1966088 | tf_op jit(solution)/shard_map/ppermute | solution.py:42
  141.5 1.2 copy-start.3

commit v4 on v3

--- a/solution.py
+++ b/solution.py
@@ -65,13 +65,15 @@
     low_rank_block = jnp.moveaxis(low_rank_block, 0, 1).reshape(gradient.shape[0], -1)
     power_part = inner_rows(gradient, low_rank_block)
     n_group = n_z * lax.axis_size("tensor")
-    halves = power_part.reshape(2, n_group, -1, power_part.shape[1])
-    own_half = lax.dynamic_index_in_dim(halves, core, axis=0, keepdims=False)
-    other_half = lax.dynamic_index_in_dim(halves, 1 - core, axis=0, keepdims=False)
-    chip_half = own_half + swap_cores(other_half)
+    width = power_part.shape[1] // 2
+    own_half = lax.dynamic_slice_in_dim(power_part, core * width, width, axis=1)
+    other_half = lax.dynamic_slice_in_dim(power_part, (1 - core) * width, width, axis=1)
+    chip_half = (own_half + swap_cores(other_half)).reshape(n_group, -1, width)
     piece = lax.all_to_all(chip_half, ("z", "tensor"), 0, 0, tiled=True).sum(axis=0)
     half = lax.all_to_all(jnp.broadcast_to(piece[None], chip_half.shape), ("z", "tensor"), 0, 0, tiled=True)
-    power = place_halves(half, swap_cores(half), core).reshape(power_part.shape)
+    half = half.reshape(-1, width)
+    partner = swap_cores(half)
+    power = jnp.where(core == 0, jnp.concatenate([half, partner], axis=1), jnp.concatenate([partner, half], axis=1))
     moment_one = 0.9 * first_moment[0, 0] + 0.1 * low_rank
     moment_two = 0.95 * second_moment[0, 0] + 0.05 * low_rank * low_rank
     direction = moment_one / (jnp.sqrt(moment_two) + 1e-08)

time: 154 us -> 139 us (0.903)
  local copies, waits for them, and re-layouts: 10.3 us -> 3.45 us
  waiting for transfers between devices: 25.9 us -> 23.1 us
  blocking collectives: 72.1 us -> 69.6 us
  matrix products: 25.1 us -> 22.8 us
    mul x2 -> x0, local copies, waits for them, and re-layouts: 3.27 us -> none  [newton_steps(): iterate = power_part * scaling]
    all_to_all x1, waiting for transfers between devices: 19.6 us -> 16.6 us  [per_device(): lax.all_to_all(jnp.broadcast_to(piece[None], chip_half.shape), ('z', 'ten...]
    all_to_all x1, blocking collectives: 25.7 us -> 23.2 us  [per_device(): lax.all_to_all(chip_half, ('z', 'tensor'), 0, 0, tiled=True).sum(axis=0)]
    dot_general x6, matrix products: 11.1 us -> 9.45 us  [matmul(): jnp.dot(left, right, precision=lax.Precision.HIGH, preferred_element_type...]
where the time goes in v4:
time: 139 us
  blocking collectives  69.6 us (50%)
  waiting for transfers between devices  23.1 us (17%)
  matrix products  22.8 us (16%)
  starting transfers between devices  15.9 us (11%)
  local copies, waits for them, and re-layouts  3.45 us (2%)
  other arithmetic  2.37 us (2%)
  between operations  1.55 us (1%)
    all_to_all x1, blocking collectives, per_device(): lax.all_to_all(chip_sum, 'z', 0, 0, tiled=True).sum(axis=0) / root_width  25.8 us
    all_to_all x1, blocking collectives, per_device(): lax.all_to_all(chip_half, ('z', 'tensor'), 0, 0, tiled=True).sum(axis=0)  23.2 us
    all_to_all x1, blocking collectives, per_device(): lax.all_to_all(jnp.broadcast_to(low_rank[None], (n_z,) + low_rank.shape),...  20.6 us
    all_to_all x1, waiting for transfers between devices, per_device(): lax.all_to_all(jnp.broadcast_to(piece[None], chip_half.shape), ('z', 'ten...  16.6 us
    dot_general x6, matrix products, inner_rows(): lax.dot_general(left, right, (((0,), (0,)), ((), ())), precision=lax.Prec...  12.5 us
    ppermute x4, starting transfers between devices, swap_cores(): return lax.ppermute(x, 'core', [(0, 1), (1, 0)])  10.3 us
    dot_general x6, matrix products, matmul(): jnp.dot(left, right, precision=lax.Precision.HIGH, preferred_element_type...  9.45 us
    ppermute x4, waiting for transfers between devices, swap_cores(): return lax.ppermute(x, 'core', [(0, 1), (1, 0)])  6.45 us
  transfers between devices with their start and end apart: 5, of which 5 were waited for; matrix products, arithmetic and copies ran while one was open for 1% of the time, Pallas kernels for 0%

profile of v4, /device:TPU:1, one launch (start us, length us, event | category | flops | bytes accessed | tf_op | source)
XLA Modules:
  0.0 138.7 jit_solution(8912764368085018517)
XLA Ops:
  0.7 1.3 copy-done
  2.0 4.9 %fusion.9 = f32[8,2,80,256]{3,2,1,0:T(8,128)S(1)} fusion(f32[8,2,80,1280]{3,2,1,0:T(8,128)} %bitcast.68, f32[1,1280,256]{2,1,0:T(8,128)S(1)} %copy-done), kind=kOutput, calls=%fused_computation.17 | convolution fusion | flops 2516582400 | bytes 9175040 | tf_op jit(solution)/shard_map/dot_general | solution.py:12
  6.8 0.9 dynamic-slice_bitcast_fusion.1
  7.8 3.2 %collective-permute-start = (f32[8,80,256]{2,1,0:T(8,128)}, f32[8,80,256]{2,1,0:T(8,128)S(1)}, u32[]{:S(2)}, u32[]{:S(2)}) collective-permute-start(f32[8,80,256]{2,1,0:T(8,128)} %dynamic-slice_bitcast_fusion.1), channel_id=1, source_target_pairs={{0,4},{4,0},{1,5},{5,1},{2,6},{6,2},{3,7},{7,3},{8,12},{12,8},{9,1... | collective-permute-start | bytes 1966088 | tf_op jit(solution)/shard_map/ppermute | solution.py:42
  11.0 1.9 %collective-permute-done = f32[8,80,256]{2,1,0:T(8,128)S(1)} collective-permute-done((f32[8,80,256]{2,1,0:T(8,128)}, f32[8,80,256]{2,1,0:T(8,128)S(1)}, u32[]{:S(2)}, u32[]{:S(2)}) %collective-permute-start) | collective-permute-done | bytes 655392 | tf_op jit(solution)/shard_map/ppermute | solution.py:42
  13.0 25.8 %all_to_all.20 = f32[8,80,256]{2,1,0:T(8,128)S(1)} all-to-all(f32[8,80,256]{2,1,0:T(8,128)S(1)} %bitcast_add_fusion.1), channel_id=1, replica_groups=mesh['section'=4,'z'=8,'core'=2,'tensor'=4] {'z'}, dimensions={0} | all-to-all | bytes 1310720 | tf_op jit(solution)/shard_map/all_to_all | solution.py:62
  38.9 20.6 %all_to_all.21 = f32[8,80,256]{2,1,0:T(8,128)S(1)} all-to-all(f32[8,80,256]{2,1,0:T(8,128)S(1)} %broadcast_in_dim.13), channel_id=1, replica_groups=mesh['section'=4,'z'=8,'core'=2,'tensor'=4] {'z'}, dimensions={0} | all-to-all | bytes 1310720 | tf_op jit(solution)/shard_map/all_to_all | solution.py:63
  59.5 3.0 %collective-permute-start.1 = (f32[8,80,256]{2,1,0:T(8,128)S(1)}, f32[8,80,256]{2,1,0:T(8,128)S(1)}, u32[]{:S(2)}, u32[]{:S(2)}) collective-permute-start(f32[8,80,256]{2,1,0:T(8,128)S(1)} %all_to_all.21), channel_id=1, source_target_pairs={{0,4},{4,0},{1,5},{5,1},{2,6},{6,2},{3,7},{7,3},{8,12},{12,8},{9,1... | collective-permute-start | bytes 1966088 | tf_op jit(solution)/shard_map/ppermute | solution.py:42
  62.6 1.7 %collective-permute-done.1 = f32[8,80,256]{2,1,0:T(8,128)S(1)} collective-permute-done((f32[8,80,256]{2,1,0:T(8,128)S(1)}, f32[8,80,256]{2,1,0:T(8,128)S(1)}, u32[]{:S(2)}, u32[]{:S(2)}) %collective-permute-start.1) | collective-permute-done | bytes 655392 | tf_op jit(solution)/shard_map/ppermute | solution.py:42
  64.5 5.8 %fusion = f32[256,1280]{1,0:T(8,128)S(1)} fusion(f32[1280,256]{1,0:T(8,128)S(1)} %bitcast.69, f32[1,1,1280,1280]{3,2,1,0:T(8,128)} %param.5), kind=kOutput, calls=%fused_computation | convolution fusion | flops 2516582400 | bytes 9175040 | tf_op jit(solution)/shard_map/dot_general | solution.py:16
  70.4 0.5 collective-permute-start.2
  70.8 1.9 %collective-permute-done.2 = f32[1280,128]{0,1:T(8,128)} collective-permute-done((f32[1280,128]{0,1:T(8,128)S(1)}, f32[1280,128]{0,1:T(8,128)}, u32[]{:S(2)}, u32[]{:S(2)}) %collective-permute-start.2) | collective-permute-done | bytes 655392 | tf_op jit(solution)/shard_map/ppermute | solution.py:42
  72.7 1.2 bitcast_add_fusion
  73.8 0.2 copy.10
  74.1 23.2 %all_to_all.22 = f32[32,40,128]{2,1,0:T(8,128)S(1)} all-to-all(f32[32,40,128]{2,1,0:T(8,128)S(1)} %bitcast.70), channel_id=1, replica_groups=mesh['section'=4,'z'=8,'core'=2,'tensor'=4] {'z','tensor'}, dimensions={0} | all-to-all | bytes 1310720 | tf_op jit(solution)/shard_map/all_to_all | solution.py:72
  97.3 0.9 broadcast_in_dim.14
  98.2 5.6 %all-to-all-start.3 = ((f32[32,40,128]{2,1,0:T(8,128)}), f32[32,40,128]{2,1,0:T(8,128)S(1)}, u32[]{:S(2)}, u32[]{:S(2)}) async-start(f32[32,40,128]{2,1,0:T(8,128)} %broadcast_in_dim.14), calls=%async_computation.3 | async-start | bytes 1310720 | tf_op jit(solution)/shard_map/all_to_all | solution.py:73
  103.9 0.8 multiply_reduce_fusion
  104.7 16.6 %all-to-all-done.3 = f32[32,40,128]{2,1,0:T(8,128)S(1)} async-done(((f32[32,40,128]{2,1,0:T(8,128)}), f32[32,40,128]{2,1,0:T(8,128)S(1)}, u32[]{:S(2)}, u32[]{:S(2)}) %all-to-all-start.3) | async-done | bytes 655392 | tf_op jit(solution)/shard_map/all_to_all | solution.py:73
  121.4 3.6 %collective-permute-start.3 = (f32[1280,128]{1,0:T(8,128)S(1)}, f32[1280,128]{1,0:T(8,128)S(1)}, u32[]{:S(2)}, u32[]{:S(2)}) collective-permute-start(f32[1280,128]{1,0:T(8,128)S(1)} %bitcast.71), channel_id=1, source_target_pairs={{0,4},{4,0},{1,5},{5,1},{2,6},{6,2},{3,7},{7,3},{8,12},{12,8},{9,1... | collective-permute-start | bytes 1966088 | tf_op jit(solution)/shard_map/ppermute | solution.py:42
  125.0 0.8 fusion.20
  125.8 0.9 collective-permute-done.3
  126.7 1.8 %select_reduce_fusion = (f32[]{:T(128)}, f32[256,256]{1,0:T(8,128)S(1)}) fusion(f32[1280,128]{1,0:T(8,128)S(1)} %collective-permute-done.3, f32[1280,128]{1,0:T(8,128)S(1)} %bitcast.72, pred[]{:T(512)S(6)} %eq.9), kind=kOutput, calls=%fused_computation.35 | convolution fusion | flops 504496128 | bytes 1572869 | tf_op jit(solution)/shard_map/dot_general | solution.py:16
  129.2 0.7 multiply_subtract_fusion
  130.0 1.3 fusion.30
  131.2 0.7 fusion.6
  131.9 1.2 fusion.31
  133.1 0.7 fusion.5
  133.8 1.2 fusion.32
  135.1 0.7 fusion.4
  135.7 1.2 fusion.33
  137.0 1.8 %fusion.7 = f32[1,1280,256]{2,1,0:T(8,128)} fusion(f32[1280,256]{1,0:T(8,128)S(1)} %fusion.4, f32[256,256]{1,0:T(8,128)S(1)} %fusion.33), kind=kOutput, calls=%fused_computation.12 | convolution fusion | flops 504627200 | bytes 2883584 | tf_op jit(solution)/shard_map/dot_general | solution.py:12
  (21 shorter events, 0.6 us)
Async XLA Ops:
  0.6 1.3 copy-start
  7.8 5.1 %collective-permute-start = (f32[8,80,256]{2,1,0:T(8,128)}, f32[8,80,256]{2,1,0:T(8,128)S(1)}, u32[]{:S(2)}, u32[]{:S(2)}) collective-permute-start(f32[8,80,256]{2,1,0:T(8,128)} %dynamic-slice_bitcast_fusion.1), channel_id=1, source_target_pairs={{0,4},{4,0},{1,5},{5,1},{2,6},{6,2},{3,7},{7,3},{8,12},{12,8},{9,1... | collective-permute-start | bytes 1966088 | tf_op jit(solution)/shard_map/ppermute | solution.py:42
  59.5 4.8 %collective-permute-start.1 = (f32[8,80,256]{2,1,0:T(8,128)S(1)}, f32[8,80,256]{2,1,0:T(8,128)S(1)}, u32[]{:S(2)}, u32[]{:S(2)}) collective-permute-start(f32[8,80,256]{2,1,0:T(8,128)S(1)} %all_to_all.21), channel_id=1, source_target_pairs={{0,4},{4,0},{1,5},{5,1},{2,6},{6,2},{3,7},{7,3},{8,12},{12,8},{9,1... | collective-permute-start | bytes 1966088 | tf_op jit(solution)/shard_map/ppermute | solution.py:42
  70.4 2.3 %collective-permute-start.2 = (f32[1280,128]{0,1:T(8,128)S(1)}, f32[1280,128]{0,1:T(8,128)}, u32[]{:S(2)}, u32[]{:S(2)}) collective-permute-start(f32[1280,128]{0,1:T(8,128)S(1)} %dynamic-slice_bitcast_fusion), channel_id=1, source_target_pairs={{0,4},{4,0},{1,5},{5,1},{2,6},{6,2},{3,7},{7,3},{8,12},{12,8},{9,1... | collective-permute-start | bytes 1966088 | tf_op jit(solution)/shard_map/ppermute | solution.py:42
  97.3 6.5 %copy-start.4 = (f32[1,1,80,256]{3,2,1,0:T(8,128)S(1)}, f32[1,1,80,256]{3,2,1,0:T(8,128)}, u32[]{:S(2)}) copy-start(f32[1,1,80,256]{3,2,1,0:T(8,128)} %param.9) | copy-start | bytes 245764
  97.3 6.6 %copy-start.5 = (f32[1,1,80,256]{3,2,1,0:T(8,128)S(1)}, f32[1,1,80,256]{3,2,1,0:T(8,128)}, u32[]{:S(2)}) copy-start(f32[1,1,80,256]{3,2,1,0:T(8,128)} %param.8) | copy-start | bytes 245764
  97.3 6.6 %copy-start.3 = (bf16[1,1,80,1280]{3,2,1,0:T(8,128)(2,1)S(1)}, bf16[1,1,80,1280]{3,2,1,0:T(8,128)(2,1)}, u32[]{:S(2)}) copy-start(bf16[1,1,80,1280]{3,2,1,0:T(8,128)(2,1)} %param.6) | copy-start | bytes 614404
  98.2 23.2 %all-to-all-start.3 = ((f32[32,40,128]{2,1,0:T(8,128)}), f32[32,40,128]{2,1,0:T(8,128)S(1)}, u32[]{:S(2)}, u32[]{:S(2)}) async-start(f32[32,40,128]{2,1,0:T(8,128)} %broadcast_in_dim.14), calls=%async_computation.3 | async-start | bytes 1310720 | tf_op jit(solution)/shard_map/all_to_all | solution.py:73
  103.9 21.9 %copy-start.1 = (f32[1,1,80,256]{3,2,1,0:T(8,128)}, f32[1,1,80,256]{3,2,1,0:T(8,128)S(1)}, u32[]{:S(2)}) copy-start(f32[1,1,80,256]{3,2,1,0:T(8,128)S(1)} %get-tuple-element.6) | copy-start | bytes 245764
  103.9 21.9 %copy-start.2 = (f32[1,1,80,256]{3,2,1,0:T(8,128)}, f32[1,1,80,256]{3,2,1,0:T(8,128)S(1)}, u32[]{:S(2)}) copy-start(f32[1,1,80,256]{3,2,1,0:T(8,128)S(1)} %get-tuple-element.7) | copy-start | bytes 245764
  121.4 5.3 %collective-permute-start.3 = (f32[1280,128]{1,0:T(8,128)S(1)}, f32[1280,128]{1,0:T(8,128)S(1)}, u32[]{:S(2)}, u32[]{:S(2)}) collective-permute-start(f32[1280,128]{1,0:T(8,128)S(1)} %bitcast.71), channel_id=1, source_target_pairs={{0,4},{4,0},{1,5},{5,1},{2,6},{6,2},{3,7},{7,3},{8,12},{12,8},{9,1... | collective-permute-start | bytes 1966088 | tf_op jit(solution)/shard_map/ppermute | solution.py:42

commit v5 on v4

--- a/solution.py
+++ b/solution.py
@@ -29,13 +29,15 @@
 def newton_steps(power_part, gram_fn):
     gram_now = gram_fn(power_part)
     scaling = lax.rsqrt(jnp.trace(gram_now) + 1e-06)
-    iterate = power_part * scaling
     gram_now = gram_now * (scaling * scaling)
+    eye = jnp.eye(gram_now.shape[0], dtype=gram_now.dtype)
+    product = None
     for sweep in range(NS_STEPS):
-        iterate = 1.5 * iterate - 0.5 * matmul(iterate, gram_now)
+        step = 1.5 * eye - 0.5 * gram_now
+        product = step if product is None else matmul(product, step)
         if sweep + 1 < NS_STEPS:
-            gram_now = gram_fn(iterate)
-    return iterate
+            gram_now = inner_rows(step, matmul(gram_now, step))
+    return matmul(power_part * scaling, product)
 
 
 def swap_cores(x):

time: 139 us -> 135 us (0.971)
  matrix products: 22.8 us -> 19 us
    dot_general x6, matrix products: 12.5 us -> 9.19 us  [inner_rows(): lax.dot_general(left, right, (((0,), (0,)), ((), ())), precision=lax.Prec...]
    dot_general x6 -> x10, matrix products: 9.45 us -> 8.99 us  [matmul(): jnp.dot(left, right, precision=lax.Precision.HIGH, preferred_element_type...]
where the time goes in v5:
time: 135 us
  blocking collectives  69.6 us (52%)
  waiting for transfers between devices  23.1 us (17%)
  matrix products  19 us (14%)
  starting transfers between devices  15.9 us (12%)
  local copies, waits for them, and re-layouts  3.45 us (3%)
  other arithmetic  2.37 us (2%)
  between operations  1.58 us (1%)
    all_to_all x1, blocking collectives, per_device(): lax.all_to_all(chip_sum, 'z', 0, 0, tiled=True).sum(axis=0) / root_width  25.8 us
    all_to_all x1, blocking collectives, per_device(): lax.all_to_all(chip_half, ('z', 'tensor'), 0, 0, tiled=True).sum(axis=0)  23.2 us
    all_to_all x1, blocking collectives, per_device(): lax.all_to_all(jnp.broadcast_to(low_rank[None], (n_z,) + low_rank.shape),...  20.6 us
    all_to_all x1, waiting for transfers between devices, per_device(): lax.all_to_all(jnp.broadcast_to(piece[None], chip_half.shape), ('z', 'ten...  16.6 us
    ppermute x4, starting transfers between devices, swap_cores(): return lax.ppermute(x, 'core', [(0, 1), (1, 0)])  10.3 us
    dot_general x6, matrix products, inner_rows(): lax.dot_general(left, right, (((0,), (0,)), ((), ())), precision=lax.Prec...  9.19 us
    dot_general x10, matrix products, matmul(): jnp.dot(left, right, precision=lax.Precision.HIGH, preferred_element_type...  8.99 us
    ppermute x4, waiting for transfers between devices, swap_cores(): return lax.ppermute(x, 'core', [(0, 1), (1, 0)])  6.45 us
  transfers between devices with their start and end apart: 5, of which 5 were waited for; matrix products, arithmetic and copies ran while one was open for 1% of the time, Pallas kernels for 0%

profile of v5, /device:TPU:1, one launch (start us, length us, event | category | flops | bytes accessed | tf_op | source)
XLA Modules:
  0.0 135.0 jit_solution(15652915591271731447)
XLA Ops:
  0.7 1.3 copy-done
  2.0 4.9 %fusion.4 = f32[8,2,80,256]{3,2,1,0:T(8,128)S(1)} fusion(f32[8,2,80,1280]{3,2,1,0:T(8,128)} %bitcast.64, f32[1,1280,256]{2,1,0:T(8,128)S(1)} %copy-done), kind=kOutput, calls=%fused_computation.8 | convolution fusion | flops 2516582400 | bytes 9175040 | tf_op jit(solution)/shard_map/dot_general | solution.py:12
  6.8 0.9 dynamic-slice_bitcast_fusion.1
  7.8 3.2 %collective-permute-start = (f32[8,80,256]{2,1,0:T(8,128)}, f32[8,80,256]{2,1,0:T(8,128)S(1)}, u32[]{:S(2)}, u32[]{:S(2)}) collective-permute-start(f32[8,80,256]{2,1,0:T(8,128)} %dynamic-slice_bitcast_fusion.1), channel_id=1, source_target_pairs={{0,4},{4,0},{1,5},{5,1},{2,6},{6,2},{3,7},{7,3},{8,12},{12,8},{9,1... | collective-permute-start | bytes 1966088 | tf_op jit(solution)/shard_map/ppermute | solution.py:44
  11.0 1.9 %collective-permute-done = f32[8,80,256]{2,1,0:T(8,128)S(1)} collective-permute-done((f32[8,80,256]{2,1,0:T(8,128)}, f32[8,80,256]{2,1,0:T(8,128)S(1)}, u32[]{:S(2)}, u32[]{:S(2)}) %collective-permute-start) | collective-permute-done | bytes 655392 | tf_op jit(solution)/shard_map/ppermute | solution.py:44
  13.0 25.8 %all_to_all.20 = f32[8,80,256]{2,1,0:T(8,128)S(1)} all-to-all(f32[8,80,256]{2,1,0:T(8,128)S(1)} %bitcast_add_fusion.1), channel_id=1, replica_groups=mesh['section'=4,'z'=8,'core'=2,'tensor'=4] {'z'}, dimensions={0} | all-to-all | bytes 1310720 | tf_op jit(solution)/shard_map/all_to_all | solution.py:64
  38.9 20.6 %all_to_all.21 = f32[8,80,256]{2,1,0:T(8,128)S(1)} all-to-all(f32[8,80,256]{2,1,0:T(8,128)S(1)} %broadcast_in_dim.13), channel_id=1, replica_groups=mesh['section'=4,'z'=8,'core'=2,'tensor'=4] {'z'}, dimensions={0} | all-to-all | bytes 1310720 | tf_op jit(solution)/shard_map/all_to_all | solution.py:65
  59.5 3.0 %collective-permute-start.1 = (f32[8,80,256]{2,1,0:T(8,128)S(1)}, f32[8,80,256]{2,1,0:T(8,128)S(1)}, u32[]{:S(2)}, u32[]{:S(2)}) collective-permute-start(f32[8,80,256]{2,1,0:T(8,128)S(1)} %all_to_all.21), channel_id=1, source_target_pairs={{0,4},{4,0},{1,5},{5,1},{2,6},{6,2},{3,7},{7,3},{8,12},{12,8},{9,1... | collective-permute-start | bytes 1966088 | tf_op jit(solution)/shard_map/ppermute | solution.py:44
  62.6 1.7 %collective-permute-done.1 = f32[8,80,256]{2,1,0:T(8,128)S(1)} collective-permute-done((f32[8,80,256]{2,1,0:T(8,128)S(1)}, f32[8,80,256]{2,1,0:T(8,128)S(1)}, u32[]{:S(2)}, u32[]{:S(2)}) %collective-permute-start.1) | collective-permute-done | bytes 655392 | tf_op jit(solution)/shard_map/ppermute | solution.py:44
  64.5 5.8 %fusion = f32[256,1280]{1,0:T(8,128)S(1)} fusion(f32[1280,256]{1,0:T(8,128)S(1)} %bitcast.65, f32[1,1,1280,1280]{3,2,1,0:T(8,128)} %param.5), kind=kOutput, calls=%fused_computation | convolution fusion | flops 2516582400 | bytes 9175040 | tf_op jit(solution)/shard_map/dot_general | solution.py:16
  70.4 0.5 collective-permute-start.2
  70.8 1.9 %collective-permute-done.2 = f32[1280,128]{0,1:T(8,128)} collective-permute-done((f32[1280,128]{0,1:T(8,128)S(1)}, f32[1280,128]{0,1:T(8,128)}, u32[]{:S(2)}, u32[]{:S(2)}) %collective-permute-start.2) | collective-permute-done | bytes 655392 | tf_op jit(solution)/shard_map/ppermute | solution.py:44
  72.7 1.2 bitcast_add_fusion
  74.1 23.2 %all_to_all.22 = f32[32,40,128]{2,1,0:T(8,128)S(1)} all-to-all(f32[32,40,128]{2,1,0:T(8,128)S(1)} %bitcast.66), channel_id=1, replica_groups=mesh['section'=4,'z'=8,'core'=2,'tensor'=4] {'z','tensor'}, dimensions={0} | all-to-all | bytes 1310720 | tf_op jit(solution)/shard_map/all_to_all | solution.py:74
  97.3 0.9 broadcast_in_dim.14
  98.2 5.6 %all-to-all-start.3 = ((f32[32,40,128]{2,1,0:T(8,128)}), f32[32,40,128]{2,1,0:T(8,128)S(1)}, u32[]{:S(2)}, u32[]{:S(2)}) async-start(f32[32,40,128]{2,1,0:T(8,128)} %broadcast_in_dim.14), calls=%async_computation.3 | async-start | bytes 1310720 | tf_op jit(solution)/shard_map/all_to_all | solution.py:75
  103.9 0.8 multiply_reduce_fusion
  104.7 16.6 %all-to-all-done.3 = f32[32,40,128]{2,1,0:T(8,128)S(1)} async-done(((f32[32,40,128]{2,1,0:T(8,128)}), f32[32,40,128]{2,1,0:T(8,128)S(1)}, u32[]{:S(2)}, u32[]{:S(2)}) %all-to-all-start.3) | async-done | bytes 655392 | tf_op jit(solution)/shard_map/all_to_all | solution.py:75
  121.4 3.6 %collective-permute-start.3 = (f32[1280,128]{1,0:T(8,128)S(1)}, f32[1280,128]{1,0:T(8,128)S(1)}, u32[]{:S(2)}, u32[]{:S(2)}) collective-permute-start(f32[1280,128]{1,0:T(8,128)S(1)} %bitcast.67), channel_id=1, source_target_pairs={{0,4},{4,0},{1,5},{5,1},{2,6},{6,2},{3,7},{7,3},{8,12},{12,8},{9,1... | collective-permute-start | bytes 1966088 | tf_op jit(solution)/shard_map/ppermute | solution.py:44
  125.0 0.8 fusion.26
  125.8 0.9 collective-permute-done.3
  126.7 1.8 %select_reduce_fusion = (f32[]{:T(128)}, f32[256,256]{1,0:T(8,128)S(1)}) fusion(f32[1280,128]{1,0:T(8,128)S(1)} %collective-permute-done.3, f32[1280,128]{1,0:T(8,128)S(1)} %bitcast.68, pred[]{:T(512)S(6)} %eq.20), kind=kOutput, calls=%fused_computation.32 | convolution fusion | flops 504496128 | bytes 1572869 | tf_op jit(solution)/shard_map/dot_general | solution.py:16
  129.2 0.3 fusion.17
  129.5 0.4 fusion.16
  130.2 0.3 fusion.15
  130.5 0.4 fusion.18
  130.9 0.3 fusion.21
  131.2 0.4 fusion.20
  131.9 0.4 fusion.8
  132.3 0.3 fusion.22
  132.6 0.3 fusion.14
  133.2 1.8 %fusion.2 = f32[1,1280,256]{2,1,0:T(8,128)} fusion(f32[256,256]{1,0:T(8,128)S(1)} %fusion.104, f32[1280,128]{1,0:T(8,128)S(1)} %collective-permute-done.3, f32[1280,128]{1,0:T(8,128)S(1)} %bitcast.69, f32[]{:T(128)S(6)} %rsqrt.12, pred[]{:T(512)S(6)} %eq.20), kind=kOutput, calls=%fused_computation.3 | convolution fusion | flops 504954880 | bytes 2883589 | tf_op jit(solution)/shard_map/dot_general | solution.py:12
  (25 shorter events, 1.6 us)
Async XLA Ops:
  0.6 1.3 copy-start
  7.8 5.1 %collective-permute-start = (f32[8,80,256]{2,1,0:T(8,128)}, f32[8,80,256]{2,1,0:T(8,128)S(1)}, u32[]{:S(2)}, u32[]{:S(2)}) collective-permute-start(f32[8,80,256]{2,1,0:T(8,128)} %dynamic-slice_bitcast_fusion.1), channel_id=1, source_target_pairs={{0,4},{4,0},{1,5},{5,1},{2,6},{6,2},{3,7},{7,3},{8,12},{12,8},{9,1... | collective-permute-start | bytes 1966088 | tf_op jit(solution)/shard_map/ppermute | solution.py:44
  59.5 4.8 %collective-permute-start.1 = (f32[8,80,256]{2,1,0:T(8,128)S(1)}, f32[8,80,256]{2,1,0:T(8,128)S(1)}, u32[]{:S(2)}, u32[]{:S(2)}) collective-permute-start(f32[8,80,256]{2,1,0:T(8,128)S(1)} %all_to_all.21), channel_id=1, source_target_pairs={{0,4},{4,0},{1,5},{5,1},{2,6},{6,2},{3,7},{7,3},{8,12},{12,8},{9,1... | collective-permute-start | bytes 1966088 | tf_op jit(solution)/shard_map/ppermute | solution.py:44
  70.4 2.3 %collective-permute-start.2 = (f32[1280,128]{0,1:T(8,128)S(1)}, f32[1280,128]{0,1:T(8,128)}, u32[]{:S(2)}, u32[]{:S(2)}) collective-permute-start(f32[1280,128]{0,1:T(8,128)S(1)} %dynamic-slice_bitcast_fusion), channel_id=1, source_target_pairs={{0,4},{4,0},{1,5},{5,1},{2,6},{6,2},{3,7},{7,3},{8,12},{12,8},{9,1... | collective-permute-start | bytes 1966088 | tf_op jit(solution)/shard_map/ppermute | solution.py:44
  97.3 6.5 %copy-start.4 = (f32[1,1,80,256]{3,2,1,0:T(8,128)S(1)}, f32[1,1,80,256]{3,2,1,0:T(8,128)}, u32[]{:S(2)}) copy-start(f32[1,1,80,256]{3,2,1,0:T(8,128)} %param.9) | copy-start | bytes 245764
  97.3 6.6 %copy-start.5 = (f32[1,1,80,256]{3,2,1,0:T(8,128)S(1)}, f32[1,1,80,256]{3,2,1,0:T(8,128)}, u32[]{:S(2)}) copy-start(f32[1,1,80,256]{3,2,1,0:T(8,128)} %param.8) | copy-start | bytes 245764
  97.3 6.6 %copy-start.3 = (bf16[1,1,80,1280]{3,2,1,0:T(8,128)(2,1)S(1)}, bf16[1,1,80,1280]{3,2,1,0:T(8,128)(2,1)}, u32[]{:S(2)}) copy-start(bf16[1,1,80,1280]{3,2,1,0:T(8,128)(2,1)} %param.6) | copy-start | bytes 614404
  98.2 23.2 %all-to-all-start.3 = ((f32[32,40,128]{2,1,0:T(8,128)}), f32[32,40,128]{2,1,0:T(8,128)S(1)}, u32[]{:S(2)}, u32[]{:S(2)}) async-start(f32[32,40,128]{2,1,0:T(8,128)} %broadcast_in_dim.14), calls=%async_computation.3 | async-start | bytes 1310720 | tf_op jit(solution)/shard_map/all_to_all | solution.py:75
  103.9 21.9 %copy-start.1 = (f32[1,1,80,256]{3,2,1,0:T(8,128)}, f32[1,1,80,256]{3,2,1,0:T(8,128)S(1)}, u32[]{:S(2)}) copy-start(f32[1,1,80,256]{3,2,1,0:T(8,128)S(1)} %get-tuple-element.6) | copy-start | bytes 245764
  103.9 21.9 %copy-start.2 = (f32[1,1,80,256]{3,2,1,0:T(8,128)}, f32[1,1,80,256]{3,2,1,0:T(8,128)S(1)}, u32[]{:S(2)}) copy-start(f32[1,1,80,256]{3,2,1,0:T(8,128)S(1)} %get-tuple-element.7) | copy-start | bytes 245764
  121.4 5.3 %collective-permute-start.3 = (f32[1280,128]{1,0:T(8,128)S(1)}, f32[1280,128]{1,0:T(8,128)S(1)}, u32[]{:S(2)}, u32[]{:S(2)}) collective-permute-start(f32[1280,128]{1,0:T(8,128)S(1)} %bitcast.67), channel_id=1, source_target_pairs={{0,4},{4,0},{1,5},{5,1},{2,6},{6,2},{3,7},{7,3},{8,12},{12,8},{9,1... | collective-permute-start | bytes 1966088 | tf_op jit(solution)/shard_map/ppermute | solution.py:44

commit v6 on v5

--- a/solution.py
+++ b/solution.py
@@ -4,6 +4,7 @@
 import jax.numpy as jnp
 from jax import lax
 from jax.sharding import Mesh, PartitionSpec as P
+
 
 NS_STEPS = 5
 
@@ -57,20 +58,22 @@
     rows = first_moment.shape[2]
     n_z = lax.axis_size("z")
     core = lax.axis_index("core")
-    partial = matmul(gradient, basis_now).reshape(n_z, 2, rows, -1)
-    own = lax.dynamic_index_in_dim(partial, core, axis=1, keepdims=False)
-    other = lax.dynamic_index_in_dim(partial, 1 - core, axis=1, keepdims=False)
-    chip_sum = own + swap_cores(other)
+    by_core = gradient.reshape(n_z, 2, rows, -1)
+    other = matmul(lax.dynamic_index_in_dim(by_core, 1 - core, axis=1, keepdims=False), basis_now)
+    sent = swap_cores(other)
+    own = lax.optimization_barrier(matmul(lax.dynamic_index_in_dim(by_core, core, axis=1, keepdims=False), basis_now))
+    chip_sum = own + sent
     low_rank = lax.all_to_all(chip_sum, "z", 0, 0, tiled=True).sum(axis=0) / root_width
     gathered = lax.all_to_all(jnp.broadcast_to(low_rank[None], (n_z,) + low_rank.shape), "z", 0, 0, tiled=True)
     low_rank_block = place_halves(gathered, swap_cores(gathered), core)
     low_rank_block = jnp.moveaxis(low_rank_block, 0, 1).reshape(gradient.shape[0], -1)
-    power_part = inner_rows(gradient, low_rank_block)
+    width = low_rank_block.shape[1] // 2
+    other_cols = lax.dynamic_slice_in_dim(low_rank_block, (1 - core) * width, width, axis=1)
+    own_cols = lax.dynamic_slice_in_dim(low_rank_block, core * width, width, axis=1)
+    sent_half = swap_cores(inner_rows(gradient, other_cols))
+    own_half = lax.optimization_barrier(inner_rows(gradient, own_cols))
     n_group = n_z * lax.axis_size("tensor")
-    width = power_part.shape[1] // 2
-    own_half = lax.dynamic_slice_in_dim(power_part, core * width, width, axis=1)
-    other_half = lax.dynamic_slice_in_dim(power_part, (1 - core) * width, width, axis=1)
-    chip_half = (own_half + swap_cores(other_half)).reshape(n_group, -1, width)
+    chip_half = (own_half + sent_half).reshape(n_group, -1, width)
     piece = lax.all_to_all(chip_half, ("z", "tensor"), 0, 0, tiled=True).sum(axis=0)
     half = lax.all_to_all(jnp.broadcast_to(piece[None], chip_half.shape), ("z", "tensor"), 0, 0, tiled=True)
     half = half.reshape(-1, width)
@@ -103,6 +106,7 @@
     devices = mesh.devices.reshape(mesh.shape["section"], -1, 2, mesh.shape["tensor"])
     split = Mesh(devices, ("section", "z", "core", "tensor"))
     shard = ("z", "core")
+
     return jax.shard_map(
         per_device,
         mesh=split,

time: 135 us -> 137 us (1.015)
  matrix products: 19 us -> 25.2 us
  waiting for transfers between devices: 23.1 us -> 19.5 us
  blocking collectives: 69.6 us -> 73.1 us
  starting transfers between devices: 15.9 us -> 13.7 us
    dot_general x6 -> x7, matrix products: 9.19 us -> 13.5 us  [inner_rows(): lax.dot_general(left, right, (((0,), (0,)), ((), ())), precision=lax.Prec...]
    ppermute x4, waiting for transfers between devices: 6.45 us -> 2.66 us  [swap_cores(): return lax.ppermute(x, 'core', [(0, 1), (1, 0)])]
    ppermute x4, starting transfers between devices: 10.3 us -> 8.38 us  [swap_cores(): return lax.ppermute(x, 'core', [(0, 1), (1, 0)])]
    dot_general x10 -> x11, matrix products: 8.99 us -> 10.9 us  [matmul(): jnp.dot(left, right, precision=lax.Precision.HIGH, preferred_element_type...]
    all_to_all x1, blocking collectives: 20.6 us -> 22.4 us  [per_device(): lax.all_to_all(jnp.broadcast_to(low_rank[None], (n_z,) + low_rank.shape),...]
  transfers between devices with their start and end apart: 5 -> 5, of which waited for: 5 -> 3; matrix products, arithmetic and copies ran while one was open for 1% -> 7% of each run, Pallas kernels for 0% -> 0%
where the time goes in v6:
time: 137 us
  blocking collectives  73.1 us (53%)
  matrix products  25.2 us (18%)
  waiting for transfers between devices  19.5 us (14%)
  starting transfers between devices  13.7 us (10%)
  local copies, waits for them, and re-layouts  2.49 us (2%)
  between operations  1.59 us (1%)
    all_to_all x1, blocking collectives, per_device(): lax.all_to_all(chip_sum, 'z', 0, 0, tiled=True).sum(axis=0) / root_width  27.1 us
    all_to_all x1, blocking collectives, per_device(): lax.all_to_all(chip_half, ('z', 'tensor'), 0, 0, tiled=True).sum(axis=0)  23.6 us
    all_to_all x1, blocking collectives, per_device(): lax.all_to_all(jnp.broadcast_to(low_rank[None], (n_z,) + low_rank.shape),...  22.4 us
    all_to_all x1, waiting for transfers between devices, per_device(): lax.all_to_all(jnp.broadcast_to(piece[None], chip_half.shape), ('z', 'ten...  16.9 us
    dot_general x7, matrix products, inner_rows(): lax.dot_general(left, right, (((0,), (0,)), ((), ())), precision=lax.Prec...  13.5 us
    dot_general x11, matrix products, matmul(): jnp.dot(left, right, precision=lax.Precision.HIGH, preferred_element_type...  10.9 us
    ppermute x4, starting transfers between devices, swap_cores(): return lax.ppermute(x, 'core', [(0, 1), (1, 0)])  8.38 us
    all_to_all x1, starting transfers between devices, per_device(): lax.all_to_all(jnp.broadcast_to(piece[None], chip_half.shape), ('z', 'ten...  5.29 us
  transfers between devices with their start and end apart: 5, of which 3 were waited for; matrix products, arithmetic and copies ran while one was open for 7% of the time, Pallas kernels for 0%

profile of v6, /device:TPU:1, one launch (start us, length us, event | category | flops | bytes accessed | tf_op | source)
XLA Modules:
  0.0 136.9 jit_solution(9376291905259967854)
XLA Ops:
  0.7 1.3 copy-done
  2.0 3.4 %fusion.4 = f32[8,80,256]{2,1,0:T(8,128)S(1)} fusion(f32[8,2,80,1280]{3,2,1,0:T(8,128)} %bitcast.73, s32[]{:T(128)S(6)} %select_n.39, f32[1,1280,256]{2,1,0:T(8,128)S(1)} %copy-done), kind=kOutput, calls=%fused_computation.4 | convolution fusion | flops 1258291200 | bytes 5242884 | tf_op jit(solution)/shard_map/dot_general | solution.py:13
  5.3 3.3 %collective-permute-start = (f32[8,80,256]{2,1,0:T(8,128)S(1)}, f32[8,80,256]{2,1,0:T(8,128)S(1)}, u32[]{:S(2)}, u32[]{:S(2)}) collective-permute-start(f32[8,80,256]{2,1,0:T(8,128)S(1)} %fusion.4), channel_id=1, source_target_pairs={{0,4},{4,0},{1,5},{5,1},{2,6},{6,2},{3,7},{7,3},{8,12},{12,8},{9,1... | collective-permute-start | bytes 1966088 | tf_op jit(solution)/shard_map/ppermute | solution.py:45
  8.6 3.4 %fusion.6 = f32[8,80,256]{2,1,0:T(8,128)S(1)} fusion(f32[8,2,80,1280]{3,2,1,0:T(8,128)} %bitcast.74, s32[]{:T(128)S(6)} %select_n.38, f32[1,1280,256]{2,1,0:T(8,128)S(1)} %copy-done), kind=kOutput, calls=%fused_computation.6 | convolution fusion | flops 1258291200 | bytes 5242884 | tf_op jit(solution)/shard_map/dot_general | solution.py:13
  12.2 27.1 %all_to_all.20 = f32[8,80,256]{2,1,0:T(8,128)S(1)} all-to-all(f32[8,80,256]{2,1,0:T(8,128)S(1)} %add.53), channel_id=1, replica_groups=mesh['section'=4,'z'=8,'core'=2,'tensor'=4] {'z'}, dimensions={0} | all-to-all | bytes 1310720 | tf_op jit(solution)/shard_map/all_to_all | solution.py:66
  39.4 22.4 %all_to_all.21 = f32[8,80,256]{2,1,0:T(8,128)S(1)} all-to-all(f32[8,80,256]{2,1,0:T(8,128)S(1)} %broadcast_in_dim.13), channel_id=1, replica_groups=mesh['section'=4,'z'=8,'core'=2,'tensor'=4] {'z'}, dimensions={0} | all-to-all | bytes 1310720 | tf_op jit(solution)/shard_map/all_to_all | solution.py:67
  61.7 1.3 collective-permute-start.1
  63.0 1.7 %collective-permute-done.1 = f32[8,80,256]{2,1,0:T(8,128)S(1)} collective-permute-done((f32[8,80,256]{2,1,0:T(8,128)S(1)}, f32[8,80,256]{2,1,0:T(8,128)S(1)}, u32[]{:S(2)}, u32[]{:S(2)}) %collective-permute-start.1) | collective-permute-done | bytes 655392 | tf_op jit(solution)/shard_map/ppermute | solution.py:45
  65.0 5.4 %fusion.14 = f32[1280,128]{0,1:T(8,128)} fusion(f32[1,1,1280,1280]{3,2,1,0:T(8,128)} %param.5, f32[1280,256]{1,0:T(8,128)S(1)} %bitcast.75, s32[]{:T(128)S(6)} %select_n.45), kind=kOutput, calls=%fused_computation.13 | convolution fusion | flops 1258291200 | bytes 7864324 | tf_op jit(solution)/shard_map/dot_general | solution.py:17
  70.4 0.5 collective-permute-start.2
  70.8 4.7 %fusion.11 = f32[1280,128]{0,1:T(8,128)S(1)} fusion(f32[1,1,1280,1280]{3,2,1,0:T(8,128)} %param.5, f32[1280,256]{1,0:T(8,128)S(1)} %bitcast.76, s32[]{:T(128)S(6)} %select_n.44), kind=kOutput, calls=%fused_computation.12 | convolution fusion | flops 1258291200 | bytes 7864324 | tf_op jit(solution)/shard_map/dot_general | solution.py:17
  75.8 23.6 %all_to_all.22 = f32[32,40,128]{2,1,0:T(8,128)S(1)} all-to-all(f32[32,40,128]{2,1,0:T(8,128)S(1)} %bitcast.77), channel_id=1, replica_groups=mesh['section'=4,'z'=8,'core'=2,'tensor'=4] {'z','tensor'}, dimensions={0} | all-to-all | bytes 1310720 | tf_op jit(solution)/shard_map/all_to_all | solution.py:77
  99.5 0.9 broadcast_in_dim.14
  100.4 5.3 %all-to-all-start.3 = ((f32[32,40,128]{2,1,0:T(8,128)}), f32[32,40,128]{2,1,0:T(8,128)S(1)}, u32[]{:S(2)}, u32[]{:S(2)}) async-start(f32[32,40,128]{2,1,0:T(8,128)} %broadcast_in_dim.14), calls=%async_computation.3 | async-start | bytes 1310720 | tf_op jit(solution)/shard_map/all_to_all | solution.py:78
  105.8 0.8 multiply_reduce_fusion
  106.7 16.9 %all-to-all-done.3 = f32[32,40,128]{2,1,0:T(8,128)S(1)} async-done(((f32[32,40,128]{2,1,0:T(8,128)}), f32[32,40,128]{2,1,0:T(8,128)S(1)}, u32[]{:S(2)}, u32[]{:S(2)}) %all-to-all-start.3) | async-done | bytes 655392 | tf_op jit(solution)/shard_map/all_to_all | solution.py:78
  123.5 3.3 %collective-permute-start.3 = (f32[1280,128]{1,0:T(8,128)S(1)}, f32[1280,128]{1,0:T(8,128)S(1)}, u32[]{:S(2)}, u32[]{:S(2)}) collective-permute-start(f32[1280,128]{1,0:T(8,128)S(1)} %bitcast.78), channel_id=1, source_target_pairs={{0,4},{4,0},{1,5},{5,1},{2,6},{6,2},{3,7},{7,3},{8,12},{12,8},{9,1... | collective-permute-start | bytes 1966088 | tf_op jit(solution)/shard_map/ppermute | solution.py:45
  126.9 0.8 fusion.42
  127.7 0.9 collective-permute-done.3
  128.6 1.8 %select_reduce_fusion = (f32[]{:T(128)}, f32[256,256]{1,0:T(8,128)S(1)}) fusion(f32[1280,128]{1,0:T(8,128)S(1)} %collective-permute-done.3, f32[1280,128]{1,0:T(8,128)S(1)} %bitcast.79, pred[]{:T(512)S(6)} %eq.20), kind=kOutput, calls=%fused_computation.40 | convolution fusion | flops 504496128 | bytes 1572869 | tf_op jit(solution)/shard_map/dot_general | solution.py:17
  131.1 0.3 fusion.33
  131.4 0.4 fusion.32
  131.8 0.3 fusion.35
  132.1 0.3 fusion.31
  132.4 0.4 fusion.34
  132.8 0.3 fusion.37
  133.1 0.4 fusion.36
  133.5 0.3 fusion.29
  133.8 0.4 fusion.22
  134.2 0.3 fusion.38
  134.5 0.3 fusion.30
  135.1 1.8 %fusion.10 = f32[1,1280,256]{2,1,0:T(8,128)} fusion(f32[256,256]{1,0:T(8,128)S(1)} %fusion.124, f32[1280,128]{1,0:T(8,128)S(1)} %collective-permute-done.3, f32[1280,128]{1,0:T(8,128)S(1)} %bitcast.80, f32[]{:T(128)S(6)} %rsqrt.12, pred[]{:T(512)S(6)} %eq.20), kind=kOutput, calls=%fused_computation.11 | convolution fusion | flops 504954880 | bytes 2883589 | tf_op jit(solution)/shard_map/dot_general | solution.py:13
  (25 shorter events, 1.1 us)
Async XLA Ops:
  0.6 1.3 copy-start
  5.3 6.7 %collective-permute-start = (f32[8,80,256]{2,1,0:T(8,128)S(1)}, f32[8,80,256]{2,1,0:T(8,128)S(1)}, u32[]{:S(2)}, u32[]{:S(2)}) collective-permute-start(f32[8,80,256]{2,1,0:T(8,128)S(1)} %fusion.4), channel_id=1, source_target_pairs={{0,4},{4,0},{1,5},{5,1},{2,6},{6,2},{3,7},{7,3},{8,12},{12,8},{9,1... | collective-permute-start | bytes 1966088 | tf_op jit(solution)/shard_map/ppermute | solution.py:45
  61.7 3.0 %collective-permute-start.1 = (f32[8,80,256]{2,1,0:T(8,128)S(1)}, f32[8,80,256]{2,1,0:T(8,128)S(1)}, u32[]{:S(2)}, u32[]{:S(2)}) collective-permute-start(f32[8,80,256]{2,1,0:T(8,128)S(1)} %all_to_all.21), channel_id=1, source_target_pairs={{0,4},{4,0},{1,5},{5,1},{2,6},{6,2},{3,7},{7,3},{8,12},{12,8},{9,1... | collective-permute-start | bytes 1966088 | tf_op jit(solution)/shard_map/ppermute | solution.py:45
  70.4 5.1 %collective-permute-start.2 = (f32[1280,128]{0,1:T(8,128)}, f32[1280,128]{0,1:T(8,128)S(1)}, u32[]{:S(2)}, u32[]{:S(2)}) collective-permute-start(f32[1280,128]{0,1:T(8,128)} %fusion.14), channel_id=1, source_target_pairs={{0,4},{4,0},{1,5},{5,1},{2,6},{6,2},{3,7},{7,3},{8,12},{12,8},{9,1... | collective-permute-start | bytes 1966088 | tf_op jit(solution)/shard_map/ppermute | solution.py:45
  99.5 6.2 %copy-start.4 = (f32[1,1,80,256]{3,2,1,0:T(8,128)S(1)}, f32[1,1,80,256]{3,2,1,0:T(8,128)}, u32[]{:S(2)}) copy-start(f32[1,1,80,256]{3,2,1,0:T(8,128)} %param.9) | copy-start | bytes 245764
  99.5 6.3 %copy-start.5 = (f32[1,1,80,256]{3,2,1,0:T(8,128)S(1)}, f32[1,1,80,256]{3,2,1,0:T(8,128)}, u32[]{:S(2)}) copy-start(f32[1,1,80,256]{3,2,1,0:T(8,128)} %param.8) | copy-start | bytes 245764
  99.5 6.3 %copy-start.3 = (bf16[1,1,80,1280]{3,2,1,0:T(8,128)(2,1)S(1)}, bf16[1,1,80,1280]{3,2,1,0:T(8,128)(2,1)}, u32[]{:S(2)}) copy-start(bf16[1,1,80,1280]{3,2,1,0:T(8,128)(2,1)} %param.6) | copy-start | bytes 614404
  100.4 23.1 %all-to-all-start.3 = ((f32[32,40,128]{2,1,0:T(8,128)}), f32[32,40,128]{2,1,0:T(8,128)S(1)}, u32[]{:S(2)}, u32[]{:S(2)}) async-start(f32[32,40,128]{2,1,0:T(8,128)} %broadcast_in_dim.14), calls=%async_computation.3 | async-start | bytes 1310720 | tf_op jit(solution)/shard_map/all_to_all | solution.py:78
  105.8 21.9 %copy-start.1 = (f32[1,1,80,256]{3,2,1,0:T(8,128)}, f32[1,1,80,256]{3,2,1,0:T(8,128)S(1)}, u32[]{:S(2)}) copy-start(f32[1,1,80,256]{3,2,1,0:T(8,128)S(1)} %get-tuple-element.6) | copy-start | bytes 245764
  105.8 21.9 %copy-start.2 = (f32[1,1,80,256]{3,2,1,0:T(8,128)}, f32[1,1,80,256]{3,2,1,0:T(8,128)S(1)}, u32[]{:S(2)}) copy-start(f32[1,1,80,256]{3,2,1,0:T(8,128)S(1)} %get-tuple-element.7) | copy-start | bytes 245764
  123.5 5.1 %collective-permute-start.3 = (f32[1280,128]{1,0:T(8,128)S(1)}, f32[1280,128]{1,0:T(8,128)S(1)}, u32[]{:S(2)}, u32[]{:S(2)}) collective-permute-start(f32[1280,128]{1,0:T(8,128)S(1)} %bitcast.78), channel_id=1, source_target_pairs={{0,4},{4,0},{1,5},{5,1},{2,6},{6,2},{3,7},{7,3},{8,12},{12,8},{9,1... | collective-permute-start | bytes 1966088 | tf_op jit(solution)/shard_map/ppermute | solution.py:45

commit v7 on v5

--- a/solution.py
+++ b/solution.py
@@ -57,10 +57,11 @@
     rows = first_moment.shape[2]
     n_z = lax.axis_size("z")
     core = lax.axis_index("core")
-    partial = matmul(gradient, basis_now).reshape(n_z, 2, rows, -1)
-    own = lax.dynamic_index_in_dim(partial, core, axis=1, keepdims=False)
-    other = lax.dynamic_index_in_dim(partial, 1 - core, axis=1, keepdims=False)
-    chip_sum = own + swap_cores(other)
+    by_core = gradient.reshape(n_z, 2, rows, -1)
+    other = matmul(lax.dynamic_index_in_dim(by_core, 1 - core, axis=1, keepdims=False), basis_now)
+    sent = swap_cores(other)
+    own = lax.optimization_barrier(matmul(lax.dynamic_index_in_dim(by_core, core, axis=1, keepdims=False), basis_now))
+    chip_sum = own + sent
     low_rank = lax.all_to_all(chip_sum, "z", 0, 0, tiled=True).sum(axis=0) / root_width
     gathered = lax.all_to_all(jnp.broadcast_to(low_rank[None], (n_z,) + low_rank.shape), "z", 0, 0, tiled=True)
     low_rank_block = place_halves(gathered, swap_cores(gathered), core)

time: 135 us -> 136 us (level)
  blocking collectives: 69.6 us -> 72.6 us
  waiting for transfers between devices: 23.1 us -> 21.2 us
  matrix products: 19 us -> 20.9 us
  starting transfers between devices: 15.9 us -> 14.2 us
    ppermute x4, waiting for transfers between devices: 6.45 us -> 4.52 us  [swap_cores(): return lax.ppermute(x, 'core', [(0, 1), (1, 0)])]
    dot_general x10 -> x11, matrix products: 8.99 us -> 10.9 us  [matmul(): jnp.dot(left, right, precision=lax.Precision.HIGH, preferred_element_type...]
    all_to_all x1, blocking collectives: 20.6 us -> 22.4 us  [per_device(): lax.all_to_all(jnp.broadcast_to(low_rank[None], (n_z,) + low_rank.shape),...]
    ppermute x4, starting transfers between devices: 10.3 us -> 8.64 us  [swap_cores(): return lax.ppermute(x, 'core', [(0, 1), (1, 0)])]
  transfers between devices with their start and end apart: 5 -> 5, of which waited for: 5 -> 4; matrix products, arithmetic and copies ran while one was open for 1% -> 4% of each run, Pallas kernels for 0% -> 0%
where the time goes in v7:
time: 136 us; the launch traced here: 135 us
  blocking collectives  72.6 us (53%)
  waiting for transfers between devices  21.2 us (16%)
  matrix products  20.9 us (15%)
  starting transfers between devices  14.2 us (10%)
  local copies, waits for them, and re-layouts  2.54 us (2%)
  other arithmetic  2.41 us (2%)
  between operations  1.59 us (1%)
    all_to_all x1, blocking collectives, per_device(): lax.all_to_all(chip_sum, 'z', 0, 0, tiled=True).sum(axis=0) / root_width  27.1 us
    all_to_all x1, blocking collectives, per_device(): lax.all_to_all(chip_half, ('z', 'tensor'), 0, 0, tiled=True).sum(axis=0)  23.2 us
    all_to_all x1, blocking collectives, per_device(): lax.all_to_all(jnp.broadcast_to(low_rank[None], (n_z,) + low_rank.shape),...  22.4 us
    all_to_all x1, waiting for transfers between devices, per_device(): lax.all_to_all(jnp.broadcast_to(piece[None], chip_half.shape), ('z', 'ten...  16.6 us
    dot_general x11, matrix products, matmul(): jnp.dot(left, right, precision=lax.Precision.HIGH, preferred_element_type...  10.9 us
    dot_general x6, matrix products, inner_rows(): lax.dot_general(left, right, (((0,), (0,)), ((), ())), precision=lax.Prec...  9.2 us
    ppermute x4, starting transfers between devices, swap_cores(): return lax.ppermute(x, 'core', [(0, 1), (1, 0)])  8.64 us
    all_to_all x1, starting transfers between devices, per_device(): lax.all_to_all(jnp.broadcast_to(piece[None], chip_half.shape), ('z', 'ten...  5.6 us
  transfers between devices with their start and end apart: 5, of which 4 were waited for; matrix products, arithmetic and copies ran while one was open for 4% of the time, Pallas kernels for 0%

profile of v7, /device:TPU:1, one launch (start us, length us, event | category | flops | bytes accessed | tf_op | source)
XLA Modules:
  0.0 135.4 jit_solution(2205361887084664362)
XLA Ops:
  0.7 1.3 copy-done
  2.0 3.4 %fusion.2 = f32[8,80,256]{2,1,0:T(8,128)S(1)} fusion(f32[8,2,80,1280]{3,2,1,0:T(8,128)} %bitcast.68, s32[]{:T(128)S(6)} %select_n.39, f32[1,1280,256]{2,1,0:T(8,128)S(1)} %copy-done), kind=kOutput, calls=%fused_computation.2 | convolution fusion | flops 1258291200 | bytes 5242884 | tf_op jit(solution)/shard_map/dot_general | solution.py:12
  5.3 3.3 %collective-permute-start = (f32[8,80,256]{2,1,0:T(8,128)S(1)}, f32[8,80,256]{2,1,0:T(8,128)S(1)}, u32[]{:S(2)}, u32[]{:S(2)}) collective-permute-start(f32[8,80,256]{2,1,0:T(8,128)S(1)} %fusion.2), channel_id=1, source_target_pairs={{0,4},{4,0},{1,5},{5,1},{2,6},{6,2},{3,7},{7,3},{8,12},{12,8},{9,1... | collective-permute-start | bytes 1966088 | tf_op jit(solution)/shard_map/ppermute | solution.py:44
  8.6 3.4 %fusion.4 = f32[8,80,256]{2,1,0:T(8,128)S(1)} fusion(f32[8,2,80,1280]{3,2,1,0:T(8,128)} %bitcast.69, s32[]{:T(128)S(6)} %select_n.38, f32[1,1280,256]{2,1,0:T(8,128)S(1)} %copy-done), kind=kOutput, calls=%fused_computation.4 | convolution fusion | flops 1258291200 | bytes 5242884 | tf_op jit(solution)/shard_map/dot_general | solution.py:12
  12.2 27.1 %all_to_all.20 = f32[8,80,256]{2,1,0:T(8,128)S(1)} all-to-all(f32[8,80,256]{2,1,0:T(8,128)S(1)} %add.53), channel_id=1, replica_groups=mesh['section'=4,'z'=8,'core'=2,'tensor'=4] {'z'}, dimensions={0} | all-to-all | bytes 1310720 | tf_op jit(solution)/shard_map/all_to_all | solution.py:65
  39.4 22.4 %all_to_all.21 = f32[8,80,256]{2,1,0:T(8,128)S(1)} all-to-all(f32[8,80,256]{2,1,0:T(8,128)S(1)} %broadcast_in_dim.13), channel_id=1, replica_groups=mesh['section'=4,'z'=8,'core'=2,'tensor'=4] {'z'}, dimensions={0} | all-to-all | bytes 1310720 | tf_op jit(solution)/shard_map/all_to_all | solution.py:66
  61.7 1.3 collective-permute-start.1
  63.0 1.7 %collective-permute-done.1 = f32[8,80,256]{2,1,0:T(8,128)S(1)} collective-permute-done((f32[8,80,256]{2,1,0:T(8,128)S(1)}, f32[8,80,256]{2,1,0:T(8,128)S(1)}, u32[]{:S(2)}, u32[]{:S(2)}) %collective-permute-start.1) | collective-permute-done | bytes 655392 | tf_op jit(solution)/shard_map/ppermute | solution.py:44
  65.0 5.8 %fusion = f32[256,1280]{1,0:T(8,128)S(1)} fusion(f32[1280,256]{1,0:T(8,128)S(1)} %bitcast.70, f32[1,1,1280,1280]{3,2,1,0:T(8,128)} %param.5), kind=kOutput, calls=%fused_computation | convolution fusion | flops 2516582400 | bytes 9175040 | tf_op jit(solution)/shard_map/dot_general | solution.py:16
  70.8 0.5 collective-permute-start.2
  71.3 1.9 %collective-permute-done.2 = f32[1280,128]{0,1:T(8,128)} collective-permute-done((f32[1280,128]{0,1:T(8,128)S(1)}, f32[1280,128]{0,1:T(8,128)}, u32[]{:S(2)}, u32[]{:S(2)}) %collective-permute-start.2) | collective-permute-done | bytes 655392 | tf_op jit(solution)/shard_map/ppermute | solution.py:44
  73.1 1.2 bitcast_add_fusion
  74.5 23.2 %all_to_all.22 = f32[32,40,128]{2,1,0:T(8,128)S(1)} all-to-all(f32[32,40,128]{2,1,0:T(8,128)S(1)} %bitcast.71), channel_id=1, replica_groups=mesh['section'=4,'z'=8,'core'=2,'tensor'=4] {'z','tensor'}, dimensions={0} | all-to-all | bytes 1310720 | tf_op jit(solution)/shard_map/all_to_all | solution.py:75
  97.8 0.9 broadcast_in_dim.14
  98.6 5.6 %all-to-all-start.3 = ((f32[32,40,128]{2,1,0:T(8,128)}), f32[32,40,128]{2,1,0:T(8,128)S(1)}, u32[]{:S(2)}, u32[]{:S(2)}) async-start(f32[32,40,128]{2,1,0:T(8,128)} %broadcast_in_dim.14), calls=%async_computation.3 | async-start | bytes 1310720 | tf_op jit(solution)/shard_map/all_to_all | solution.py:76
  104.3 0.8 multiply_reduce_fusion
  105.2 16.6 %all-to-all-done.3 = f32[32,40,128]{2,1,0:T(8,128)S(1)} async-done(((f32[32,40,128]{2,1,0:T(8,128)}), f32[32,40,128]{2,1,0:T(8,128)S(1)}, u32[]{:S(2)}, u32[]{:S(2)}) %all-to-all-start.3) | async-done | bytes 655392 | tf_op jit(solution)/shard_map/all_to_all | solution.py:76
  121.8 3.6 %collective-permute-start.3 = (f32[1280,128]{1,0:T(8,128)S(1)}, f32[1280,128]{1,0:T(8,128)S(1)}, u32[]{:S(2)}, u32[]{:S(2)}) collective-permute-start(f32[1280,128]{1,0:T(8,128)S(1)} %bitcast.72), channel_id=1, source_target_pairs={{0,4},{4,0},{1,5},{5,1},{2,6},{6,2},{3,7},{7,3},{8,12},{12,8},{9,1... | collective-permute-start | bytes 1966088 | tf_op jit(solution)/shard_map/ppermute | solution.py:44
  125.4 0.8 fusion.32
  126.2 0.9 collective-permute-done.3
  127.2 1.8 %select_reduce_fusion = (f32[]{:T(128)}, f32[256,256]{1,0:T(8,128)S(1)}) fusion(f32[1280,128]{1,0:T(8,128)S(1)} %collective-permute-done.3, f32[1280,128]{1,0:T(8,128)S(1)} %bitcast.73, pred[]{:T(512)S(6)} %eq.20), kind=kOutput, calls=%fused_computation.36 | convolution fusion | flops 504496128 | bytes 1572869 | tf_op jit(solution)/shard_map/dot_general | solution.py:16
  129.7 0.3 fusion.23
  130.0 0.4 fusion.22
  130.4 0.3 fusion.25
  130.7 0.3 fusion.21
  131.0 0.4 fusion.24
  131.7 0.4 fusion.26
  132.1 0.3 fusion.19
  132.4 0.4 fusion.14
  132.8 0.3 fusion.28
  133.1 0.3 fusion.20
  133.7 1.8 %fusion.8 = f32[1,1280,256]{2,1,0:T(8,128)} fusion(f32[256,256]{1,0:T(8,128)S(1)} %fusion.112, f32[1280,128]{1,0:T(8,128)S(1)} %collective-permute-done.3, f32[1280,128]{1,0:T(8,128)S(1)} %bitcast.74, f32[]{:T(128)S(6)} %rsqrt.12, pred[]{:T(512)S(6)} %eq.20), kind=kOutput, calls=%fused_computation.9 | convolution fusion | flops 504954880 | bytes 2883589 | tf_op jit(solution)/shard_map/dot_general | solution.py:12
  (25 shorter events, 1.4 us)
Async XLA Ops:
  0.6 1.3 copy-start
  5.3 6.7 %collective-permute-start = (f32[8,80,256]{2,1,0:T(8,128)S(1)}, f32[8,80,256]{2,1,0:T(8,128)S(1)}, u32[]{:S(2)}, u32[]{:S(2)}) collective-permute-start(f32[8,80,256]{2,1,0:T(8,128)S(1)} %fusion.2), channel_id=1, source_target_pairs={{0,4},{4,0},{1,5},{5,1},{2,6},{6,2},{3,7},{7,3},{8,12},{12,8},{9,1... | collective-permute-start | bytes 1966088 | tf_op jit(solution)/shard_map/ppermute | solution.py:44
  61.7 3.0 %collective-permute-start.1 = (f32[8,80,256]{2,1,0:T(8,128)S(1)}, f32[8,80,256]{2,1,0:T(8,128)S(1)}, u32[]{:S(2)}, u32[]{:S(2)}) collective-permute-start(f32[8,80,256]{2,1,0:T(8,128)S(1)} %all_to_all.21), channel_id=1, source_target_pairs={{0,4},{4,0},{1,5},{5,1},{2,6},{6,2},{3,7},{7,3},{8,12},{12,8},{9,1... | collective-permute-start | bytes 1966088 | tf_op jit(solution)/shard_map/ppermute | solution.py:44
  70.8 2.3 %collective-permute-start.2 = (f32[1280,128]{0,1:T(8,128)S(1)}, f32[1280,128]{0,1:T(8,128)}, u32[]{:S(2)}, u32[]{:S(2)}) collective-permute-start(f32[1280,128]{0,1:T(8,128)S(1)} %dynamic-slice_bitcast_fusion), channel_id=1, source_target_pairs={{0,4},{4,0},{1,5},{5,1},{2,6},{6,2},{3,7},{7,3},{8,12},{12,8},{9,1... | collective-permute-start | bytes 1966088 | tf_op jit(solution)/shard_map/ppermute | solution.py:44
  97.7 6.6 %copy-start.4 = (f32[1,1,80,256]{3,2,1,0:T(8,128)S(1)}, f32[1,1,80,256]{3,2,1,0:T(8,128)}, u32[]{:S(2)}) copy-start(f32[1,1,80,256]{3,2,1,0:T(8,128)} %param.9) | copy-start | bytes 245764
  97.7 6.6 %copy-start.5 = (f32[1,1,80,256]{3,2,1,0:T(8,128)S(1)}, f32[1,1,80,256]{3,2,1,0:T(8,128)}, u32[]{:S(2)}) copy-start(f32[1,1,80,256]{3,2,1,0:T(8,128)} %param.8) | copy-start | bytes 245764
  97.8 6.6 %copy-start.3 = (bf16[1,1,80,1280]{3,2,1,0:T(8,128)(2,1)S(1)}, bf16[1,1,80,1280]{3,2,1,0:T(8,128)(2,1)}, u32[]{:S(2)}) copy-start(bf16[1,1,80,1280]{3,2,1,0:T(8,128)(2,1)} %param.6) | copy-start | bytes 614404
  98.6 23.2 %all-to-all-start.3 = ((f32[32,40,128]{2,1,0:T(8,128)}), f32[32,40,128]{2,1,0:T(8,128)S(1)}, u32[]{:S(2)}, u32[]{:S(2)}) async-start(f32[32,40,128]{2,1,0:T(8,128)} %broadcast_in_dim.14), calls=%async_computation.3 | async-start | bytes 1310720 | tf_op jit(solution)/shard_map/all_to_all | solution.py:76
  104.3 21.9 %copy-start.1 = (f32[1,1,80,256]{3,2,1,0:T(8,128)}, f32[1,1,80,256]{3,2,1,0:T(8,128)S(1)}, u32[]{:S(2)}) copy-start(f32[1,1,80,256]{3,2,1,0:T(8,128)S(1)} %get-tuple-element.6) | copy-start | bytes 245764
  104.3 21.9 %copy-start.2 = (f32[1,1,80,256]{3,2,1,0:T(8,128)}, f32[1,1,80,256]{3,2,1,0:T(8,128)S(1)}, u32[]{:S(2)}) copy-start(f32[1,1,80,256]{3,2,1,0:T(8,128)S(1)} %get-tuple-element.7) | copy-start | bytes 245764
  121.8 5.3 %collective-permute-start.3 = (f32[1280,128]{1,0:T(8,128)S(1)}, f32[1280,128]{1,0:T(8,128)S(1)}, u32[]{:S(2)}, u32[]{:S(2)}) collective-permute-start(f32[1280,128]{1,0:T(8,128)S(1)} %bitcast.72), channel_id=1, source_target_pairs={{0,4},{4,0},{1,5},{5,1},{2,6},{6,2},{3,7},{7,3},{8,12},{12,8},{9,1... | collective-permute-start | bytes 1966088 | tf_op jit(solution)/shard_map/ppermute | solution.py:44

commit v8 on v5

--- a/solution.py
+++ b/solution.py
@@ -62,9 +62,9 @@
     other = lax.dynamic_index_in_dim(partial, 1 - core, axis=1, keepdims=False)
     chip_sum = own + swap_cores(other)
     low_rank = lax.all_to_all(chip_sum, "z", 0, 0, tiled=True).sum(axis=0) / root_width
-    gathered = lax.all_to_all(jnp.broadcast_to(low_rank[None], (n_z,) + low_rank.shape), "z", 0, 0, tiled=True)
-    low_rank_block = place_halves(gathered, swap_cores(gathered), core)
-    low_rank_block = jnp.moveaxis(low_rank_block, 0, 1).reshape(gradient.shape[0], -1)
+    low_rank_block = lax.all_to_all(
+        jnp.broadcast_to(low_rank[None], (2 * n_z,) + low_rank.shape), ("z", "core"), 0, 0, tiled=True
+    ).reshape(gradient.shape[0], -1)
     power_part = inner_rows(gradient, low_rank_block)
     n_group = n_z * lax.axis_size("tensor")
     width = power_part.shape[1] // 2

time: 135 us -> 152 us (1.13)
  waiting for transfers between devices: 23.1 us -> 55 us
  blocking collectives: 69.6 us -> 50.5 us
  local copies, waits for them, and re-layouts: 3.45 us -> 5.64 us
  starting transfers between devices: 15.9 us -> 17.7 us
    all_to_all x0 -> x1, waiting for transfers between devices: none -> 33.3 us  [per_device(): lax.all_to_all(jnp.broadcast_to(low_rank[None], (2 * n_z,) + low_rank.sha...]
    all_to_all x1 -> x0, blocking collectives: 20.6 us -> none  [per_device(): lax.all_to_all(jnp.broadcast_to(low_rank[None], (n_z,) + low_rank.shape),...]
    all_to_all x0 -> x1, starting transfers between devices: none -> 5.21 us  [per_device(): lax.all_to_all(jnp.broadcast_to(low_rank[None], (2 * n_z,) + low_rank.sha...]
    ppermute x4 -> x3, starting transfers between devices: 10.3 us -> 6.89 us  [swap_cores(): return lax.ppermute(x, 'core', [(0, 1), (1, 0)])]
    all_to_all x1, blocking collectives: 23.2 us -> 24.7 us  [per_device(): lax.all_to_all(chip_half, ('z', 'tensor'), 0, 0, tiled=True).sum(axis=0)]
    ppermute x4 -> x3, waiting for transfers between devices: 6.45 us -> 5.08 us  [swap_cores(): return lax.ppermute(x, 'core', [(0, 1), (1, 0)])]
where the time goes in v8:
time: 152 us
  waiting for transfers between devices  55 us (36%)
  blocking collectives  50.5 us (33%)
  matrix products  19.4 us (13%)
  starting transfers between devices  17.7 us (12%)
  local copies, waits for them, and re-layouts  5.64 us (4%)
  other arithmetic  2.16 us (1%)
  between operations  1.57 us (1%)
    all_to_all x1, waiting for transfers between devices, per_device(): lax.all_to_all(jnp.broadcast_to(low_rank[None], (2 * n_z,) + low_rank.sha...  33.3 us
    all_to_all x1, blocking collectives, per_device(): lax.all_to_all(chip_sum, 'z', 0, 0, tiled=True).sum(axis=0) / root_width  25.8 us
    all_to_all x1, blocking collectives, per_device(): lax.all_to_all(chip_half, ('z', 'tensor'), 0, 0, tiled=True).sum(axis=0)  24.7 us
    all_to_all x1, waiting for transfers between devices, per_device(): lax.all_to_all(jnp.broadcast_to(piece[None], chip_half.shape), ('z', 'ten...  16.6 us
    dot_general x6, matrix products, inner_rows(): lax.dot_general(left, right, (((0,), (0,)), ((), ())), precision=lax.Prec...  9.61 us
    dot_general x10, matrix products, matmul(): jnp.dot(left, right, precision=lax.Precision.HIGH, preferred_element_type...  8.98 us
    ppermute x3, starting transfers between devices, swap_cores(): return lax.ppermute(x, 'core', [(0, 1), (1, 0)])  6.89 us
    all_to_all x1, starting transfers between devices, per_device(): lax.all_to_all(jnp.broadcast_to(piece[None], chip_half.shape), ('z', 'ten...  5.59 us
  transfers between devices with their start and end apart: 5, of which 5 were waited for; matrix products, arithmetic and copies ran while one was open for 1% of the time, Pallas kernels for 0%

profile of v8, /device:TPU:1, one launch (start us, length us, event | category | flops | bytes accessed | tf_op | source)
XLA Modules:
  0.0 152.1 jit_solution(14547623509587852064)
XLA Ops:
  0.7 1.3 copy-done
  2.0 4.9 %fusion.4 = f32[8,2,80,256]{3,2,1,0:T(8,128)S(1)} fusion(f32[8,2,80,1280]{3,2,1,0:T(8,128)} %bitcast.56, f32[1,1280,256]{2,1,0:T(8,128)S(1)} %copy-done), kind=kOutput, calls=%fused_computation.7 | convolution fusion | flops 2516582400 | bytes 9175040 | tf_op jit(solution)/shard_map/dot_general | solution.py:12
  6.8 0.9 dynamic-slice_bitcast_fusion.1
  7.8 3.2 %collective-permute-start = (f32[8,80,256]{2,1,0:T(8,128)}, f32[8,80,256]{2,1,0:T(8,128)S(1)}, u32[]{:S(2)}, u32[]{:S(2)}) collective-permute-start(f32[8,80,256]{2,1,0:T(8,128)} %dynamic-slice_bitcast_fusion.1), channel_id=1, source_target_pairs={{0,4},{4,0},{1,5},{5,1},{2,6},{6,2},{3,7},{7,3},{8,12},{12,8},{9,1... | collective-permute-start | bytes 1966088 | tf_op jit(solution)/shard_map/ppermute | solution.py:44
  11.0 1.9 %collective-permute-done = f32[8,80,256]{2,1,0:T(8,128)S(1)} collective-permute-done((f32[8,80,256]{2,1,0:T(8,128)}, f32[8,80,256]{2,1,0:T(8,128)S(1)}, u32[]{:S(2)}, u32[]{:S(2)}) %collective-permute-start) | collective-permute-done | bytes 655392 | tf_op jit(solution)/shard_map/ppermute | solution.py:44
  13.0 25.8 %all_to_all.20 = f32[8,80,256]{2,1,0:T(8,128)S(1)} all-to-all(f32[8,80,256]{2,1,0:T(8,128)S(1)} %bitcast_add_fusion.1), channel_id=1, replica_groups=mesh['section'=4,'z'=8,'core'=2,'tensor'=4] {'z'}, dimensions={0} | all-to-all | bytes 1310720 | tf_op jit(solution)/shard_map/all_to_all | solution.py:64
  38.9 1.2 broadcast_in_dim.13
  40.0 5.2 %all-to-all-start.1 = ((f32[16,80,256]{2,1,0:T(8,128)}), f32[16,80,256]{2,1,0:T(8,128)S(1)}, u32[]{:S(2)}, u32[]{:S(2)}) async-start(f32[16,80,256]{2,1,0:T(8,128)} %broadcast_in_dim.13), calls=%async_computation.1 | async-start | bytes 2621440 | tf_op jit(solution)/shard_map/all_to_all | solution.py:65
  45.3 33.3 %all-to-all-done.1 = f32[16,80,256]{2,1,0:T(8,128)S(1)} async-done(((f32[16,80,256]{2,1,0:T(8,128)}), f32[16,80,256]{2,1,0:T(8,128)S(1)}, u32[]{:S(2)}, u32[]{:S(2)}) %all-to-all-start.1) | async-done | bytes 1310752 | tf_op jit(solution)/shard_map/all_to_all | solution.py:65
  78.6 1.1 copy-done.1
  79.6 6.2 %fusion = f32[256,1280]{1,0:T(8,128)S(1)} fusion(f32[1280,256]{1,0:T(8,128)} %bitcast.57, f32[1,1,1280,1280]{3,2,1,0:T(8,128)} %param.5), kind=kOutput, calls=%fused_computation | convolution fusion | flops 2516582400 | bytes 9175040 | tf_op jit(solution)/shard_map/dot_general | solution.py:16
  86.0 2.2 %collective-permute-done.1 = f32[1280,128]{0,1:T(8,128)} collective-permute-done((f32[1280,128]{0,1:T(8,128)S(1)}, f32[1280,128]{0,1:T(8,128)}, u32[]{:S(2)}, u32[]{:S(2)}) %collective-permute-start.1) | collective-permute-done | bytes 655392 | tf_op jit(solution)/shard_map/ppermute | solution.py:44
  88.2 1.2 bitcast_add_fusion
  89.6 24.7 %all_to_all.21 = f32[32,40,128]{2,1,0:T(8,128)S(1)} all-to-all(f32[32,40,128]{2,1,0:T(8,128)S(1)} %bitcast.58), channel_id=1, replica_groups=mesh['section'=4,'z'=8,'core'=2,'tensor'=4] {'z','tensor'}, dimensions={0} | all-to-all | bytes 1310720 | tf_op jit(solution)/shard_map/all_to_all | solution.py:74
  114.4 0.9 broadcast_in_dim.14
  115.3 5.6 %all-to-all-start.3 = ((f32[32,40,128]{2,1,0:T(8,128)}), f32[32,40,128]{2,1,0:T(8,128)S(1)}, u32[]{:S(2)}, u32[]{:S(2)}) async-start(f32[32,40,128]{2,1,0:T(8,128)} %broadcast_in_dim.14), calls=%async_computation.3 | async-start | bytes 1310720 | tf_op jit(solution)/shard_map/all_to_all | solution.py:75
  121.0 0.8 multiply_reduce_fusion
  121.8 16.6 %all-to-all-done.3 = f32[32,40,128]{2,1,0:T(8,128)S(1)} async-done(((f32[32,40,128]{2,1,0:T(8,128)}), f32[32,40,128]{2,1,0:T(8,128)S(1)}, u32[]{:S(2)}, u32[]{:S(2)}) %all-to-all-start.3) | async-done | bytes 655392 | tf_op jit(solution)/shard_map/all_to_all | solution.py:75
  138.5 3.6 %collective-permute-start.2 = (f32[1280,128]{1,0:T(8,128)S(1)}, f32[1280,128]{1,0:T(8,128)S(1)}, u32[]{:S(2)}, u32[]{:S(2)}) collective-permute-start(f32[1280,128]{1,0:T(8,128)S(1)} %bitcast.59), channel_id=1, source_target_pairs={{0,4},{4,0},{1,5},{5,1},{2,6},{6,2},{3,7},{7,3},{8,12},{12,8},{9,1... | collective-permute-start | bytes 1966088 | tf_op jit(solution)/shard_map/ppermute | solution.py:44
  142.1 0.8 fusion.26
  142.8 0.9 collective-permute-done.2
  143.8 1.8 %select_reduce_fusion = (f32[]{:T(128)}, f32[256,256]{1,0:T(8,128)S(1)}) fusion(f32[1280,128]{1,0:T(8,128)S(1)} %collective-permute-done.2, f32[1280,128]{1,0:T(8,128)S(1)} %bitcast.60, pred[]{:T(512)S(6)} %eq.18), kind=kOutput, calls=%fused_computation.29 | convolution fusion | flops 504496128 | bytes 1572869 | tf_op jit(solution)/shard_map/dot_general | solution.py:16
  146.3 0.3 fusion.17
  146.6 0.4 fusion.16
  147.0 0.3 fusion.19
  147.3 0.3 fusion.15
  147.6 0.4 fusion.18
  148.3 0.4 fusion.20
  149.0 0.4 fusion.8
  149.4 0.3 fusion.22
  149.7 0.3 fusion.14
  150.3 1.8 %fusion.2 = f32[1,1280,256]{2,1,0:T(8,128)} fusion(f32[256,256]{1,0:T(8,128)S(1)} %fusion.104, f32[1280,128]{1,0:T(8,128)S(1)} %collective-permute-done.2, f32[1280,128]{1,0:T(8,128)S(1)} %bitcast.61, f32[]{:T(128)S(6)} %rsqrt.12, pred[]{:T(512)S(6)} %eq.18), kind=kOutput, calls=%fused_computation.3 | convolution fusion | flops 504954880 | bytes 2883589 | tf_op jit(solution)/shard_map/dot_general | solution.py:12
  (24 shorter events, 1.5 us)
Async XLA Ops:
  0.6 1.3 copy-start
  7.8 5.1 %collective-permute-start = (f32[8,80,256]{2,1,0:T(8,128)}, f32[8,80,256]{2,1,0:T(8,128)S(1)}, u32[]{:S(2)}, u32[]{:S(2)}) collective-permute-start(f32[8,80,256]{2,1,0:T(8,128)} %dynamic-slice_bitcast_fusion.1), channel_id=1, source_target_pairs={{0,4},{4,0},{1,5},{5,1},{2,6},{6,2},{3,7},{7,3},{8,12},{12,8},{9,1... | collective-permute-start | bytes 1966088 | tf_op jit(solution)/shard_map/ppermute | solution.py:44
  40.0 38.5 %all-to-all-start.1 = ((f32[16,80,256]{2,1,0:T(8,128)}), f32[16,80,256]{2,1,0:T(8,128)S(1)}, u32[]{:S(2)}, u32[]{:S(2)}) async-start(f32[16,80,256]{2,1,0:T(8,128)} %broadcast_in_dim.13), calls=%async_computation.1 | async-start | bytes 2621440 | tf_op jit(solution)/shard_map/all_to_all | solution.py:65
  78.6 1.1 copy-start.1
  85.9 2.3 %collective-permute-start.1 = (f32[1280,128]{0,1:T(8,128)S(1)}, f32[1280,128]{0,1:T(8,128)}, u32[]{:S(2)}, u32[]{:S(2)}) collective-permute-start(f32[1280,128]{0,1:T(8,128)S(1)} %dynamic-slice_bitcast_fusion), channel_id=1, source_target_pairs={{0,4},{4,0},{1,5},{5,1},{2,6},{6,2},{3,7},{7,3},{8,12},{12,8},{9,1... | collective-permute-start | bytes 1966088 | tf_op jit(solution)/shard_map/ppermute | solution.py:44
  114.3 6.6 %copy-start.5 = (f32[1,1,80,256]{3,2,1,0:T(8,128)S(1)}, f32[1,1,80,256]{3,2,1,0:T(8,128)}, u32[]{:S(2)}) copy-start(f32[1,1,80,256]{3,2,1,0:T(8,128)} %param.9) | copy-start | bytes 245764
  114.3 6.6 %copy-start.6 = (f32[1,1,80,256]{3,2,1,0:T(8,128)S(1)}, f32[1,1,80,256]{3,2,1,0:T(8,128)}, u32[]{:S(2)}) copy-start(f32[1,1,80,256]{3,2,1,0:T(8,128)} %param.8) | copy-start | bytes 245764
  114.4 6.6 %copy-start.4 = (bf16[1,1,80,1280]{3,2,1,0:T(8,128)(2,1)S(1)}, bf16[1,1,80,1280]{3,2,1,0:T(8,128)(2,1)}, u32[]{:S(2)}) copy-start(bf16[1,1,80,1280]{3,2,1,0:T(8,128)(2,1)} %param.6) | copy-start | bytes 614404
  115.3 23.2 %all-to-all-start.3 = ((f32[32,40,128]{2,1,0:T(8,128)}), f32[32,40,128]{2,1,0:T(8,128)S(1)}, u32[]{:S(2)}, u32[]{:S(2)}) async-start(f32[32,40,128]{2,1,0:T(8,128)} %broadcast_in_dim.14), calls=%async_computation.3 | async-start | bytes 1310720 | tf_op jit(solution)/shard_map/all_to_all | solution.py:75
  120.9 21.9 %copy-start.2 = (f32[1,1,80,256]{3,2,1,0:T(8,128)}, f32[1,1,80,256]{3,2,1,0:T(8,128)S(1)}, u32[]{:S(2)}) copy-start(f32[1,1,80,256]{3,2,1,0:T(8,128)S(1)} %get-tuple-element.4) | copy-start | bytes 245764
  120.9 21.9 %copy-start.3 = (f32[1,1,80,256]{3,2,1,0:T(8,128)}, f32[1,1,80,256]{3,2,1,0:T(8,128)S(1)}, u32[]{:S(2)}) copy-start(f32[1,1,80,256]{3,2,1,0:T(8,128)S(1)} %get-tuple-element.5) | copy-start | bytes 245764
  138.5 5.3 %collective-permute-start.2 = (f32[1280,128]{1,0:T(8,128)S(1)}, f32[1280,128]{1,0:T(8,128)S(1)}, u32[]{:S(2)}, u32[]{:S(2)}) collective-permute-start(f32[1280,128]{1,0:T(8,128)S(1)} %bitcast.59), channel_id=1, source_target_pairs={{0,4},{4,0},{1,5},{5,1},{2,6},{6,2},{3,7},{7,3},{8,12},{12,8},{9,1... | collective-permute-start | bytes 1966088 | tf_op jit(solution)/shard_map/ppermute | solution.py:44

commit v9 on v5

--- a/solution.py
+++ b/solution.py
@@ -37,7 +37,7 @@
         product = step if product is None else matmul(product, step)
         if sweep + 1 < NS_STEPS:
             gram_now = inner_rows(step, matmul(gram_now, step))
-    return matmul(power_part * scaling, product)
+    return matmul(power_part, product * (scaling * math.sqrt(power_part.shape[0])))
 
 
 def swap_cores(x):
@@ -90,7 +90,7 @@
     normed = stepped * lax.rsqrt(jnp.mean(stepped * stepped, axis=1, keepdims=True) + 1e-06)
     new_weights = normed.astype(jnp.bfloat16)
     iterate = newton_steps(power, local_gram)
-    new_basis = iterate * root_width
+    new_basis = iterate
     return (
         new_weights[None, None],
         moment_one[None, None],

time: 135 us -> 135 us (level)
  no operation moved by 1% of the time
where the time goes in v9:
time: 135 us
  blocking collectives  69.6 us (52%)
  waiting for transfers between devices  23.1 us (17%)
  matrix products  19 us (14%)
  starting transfers between devices  15.9 us (12%)
  local copies, waits for them, and re-layouts  3.45 us (3%)
  other arithmetic  2.37 us (2%)
  between operations  1.58 us (1%)
    all_to_all x1, blocking collectives, per_device(): lax.all_to_all(chip_sum, 'z', 0, 0, tiled=True).sum(axis=0) / root_width  25.8 us
    all_to_all x1, blocking collectives, per_device(): lax.all_to_all(chip_half, ('z', 'tensor'), 0, 0, tiled=True).sum(axis=0)  23.2 us
    all_to_all x1, blocking collectives, per_device(): lax.all_to_all(jnp.broadcast_to(low_rank[None], (n_z,) + low_rank.shape),...  20.6 us
    all_to_all x1, waiting for transfers between devices, per_device(): lax.all_to_all(jnp.broadcast_to(piece[None], chip_half.shape), ('z', 'ten...  16.6 us
    ppermute x4, starting transfers between devices, swap_cores(): return lax.ppermute(x, 'core', [(0, 1), (1, 0)])  10.3 us
    dot_general x6, matrix products, inner_rows(): lax.dot_general(left, right, (((0,), (0,)), ((), ())), precision=lax.Prec...  9.18 us
    dot_general x10, matrix products, matmul(): jnp.dot(left, right, precision=lax.Precision.HIGH, preferred_element_type...  8.95 us
    ppermute x4, waiting for transfers between devices, swap_cores(): return lax.ppermute(x, 'core', [(0, 1), (1, 0)])  6.45 us
  transfers between devices with their start and end apart: 5, of which 5 were waited for; matrix products, arithmetic and copies ran while one was open for 1% of the time, Pallas kernels for 0%

profile of v9, /device:TPU:1, one launch (start us, length us, event | category | flops | bytes accessed | tf_op | source)
XLA Modules:
  0.0 134.9 jit_solution(15165628660906755076)
XLA Ops:
  0.7 1.3 copy-done
  2.0 4.9 %fusion.3 = f32[8,2,80,256]{3,2,1,0:T(8,128)S(1)} fusion(f32[8,2,80,1280]{3,2,1,0:T(8,128)} %bitcast.64, f32[1,1280,256]{2,1,0:T(8,128)S(1)} %copy-done), kind=kOutput, calls=%fused_computation.7 | convolution fusion | flops 2516582400 | bytes 9175040 | tf_op jit(solution)/shard_map/dot_general | solution.py:12
  6.8 0.9 dynamic-slice_bitcast_fusion.1
  7.8 3.2 %collective-permute-start = (f32[8,80,256]{2,1,0:T(8,128)}, f32[8,80,256]{2,1,0:T(8,128)S(1)}, u32[]{:S(2)}, u32[]{:S(2)}) collective-permute-start(f32[8,80,256]{2,1,0:T(8,128)} %dynamic-slice_bitcast_fusion.1), channel_id=1, source_target_pairs={{0,4},{4,0},{1,5},{5,1},{2,6},{6,2},{3,7},{7,3},{8,12},{12,8},{9,1... | collective-permute-start | bytes 1966088 | tf_op jit(solution)/shard_map/ppermute | solution.py:44
  11.0 1.9 %collective-permute-done = f32[8,80,256]{2,1,0:T(8,128)S(1)} collective-permute-done((f32[8,80,256]{2,1,0:T(8,128)}, f32[8,80,256]{2,1,0:T(8,128)S(1)}, u32[]{:S(2)}, u32[]{:S(2)}) %collective-permute-start) | collective-permute-done | bytes 655392 | tf_op jit(solution)/shard_map/ppermute | solution.py:44
  13.0 25.8 %all_to_all.20 = f32[8,80,256]{2,1,0:T(8,128)S(1)} all-to-all(f32[8,80,256]{2,1,0:T(8,128)S(1)} %bitcast_add_fusion.1), channel_id=1, replica_groups=mesh['section'=4,'z'=8,'core'=2,'tensor'=4] {'z'}, dimensions={0} | all-to-all | bytes 1310720 | tf_op jit(solution)/shard_map/all_to_all | solution.py:64
  38.9 20.6 %all_to_all.21 = f32[8,80,256]{2,1,0:T(8,128)S(1)} all-to-all(f32[8,80,256]{2,1,0:T(8,128)S(1)} %broadcast_in_dim.11), channel_id=1, replica_groups=mesh['section'=4,'z'=8,'core'=2,'tensor'=4] {'z'}, dimensions={0} | all-to-all | bytes 1310720 | tf_op jit(solution)/shard_map/all_to_all | solution.py:65
  59.5 3.0 %collective-permute-start.1 = (f32[8,80,256]{2,1,0:T(8,128)S(1)}, f32[8,80,256]{2,1,0:T(8,128)S(1)}, u32[]{:S(2)}, u32[]{:S(2)}) collective-permute-start(f32[8,80,256]{2,1,0:T(8,128)S(1)} %all_to_all.21), channel_id=1, source_target_pairs={{0,4},{4,0},{1,5},{5,1},{2,6},{6,2},{3,7},{7,3},{8,12},{12,8},{9,1... | collective-permute-start | bytes 1966088 | tf_op jit(solution)/shard_map/ppermute | solution.py:44
  62.6 1.7 %collective-permute-done.1 = f32[8,80,256]{2,1,0:T(8,128)S(1)} collective-permute-done((f32[8,80,256]{2,1,0:T(8,128)S(1)}, f32[8,80,256]{2,1,0:T(8,128)S(1)}, u32[]{:S(2)}, u32[]{:S(2)}) %collective-permute-start.1) | collective-permute-done | bytes 655392 | tf_op jit(solution)/shard_map/ppermute | solution.py:44
  64.5 5.8 %fusion = f32[256,1280]{1,0:T(8,128)S(1)} fusion(f32[1280,256]{1,0:T(8,128)S(1)} %bitcast.65, f32[1,1,1280,1280]{3,2,1,0:T(8,128)} %param.5), kind=kOutput, calls=%fused_computation | convolution fusion | flops 2516582400 | bytes 9175040 | tf_op jit(solution)/shard_map/dot_general | solution.py:16
  70.4 0.5 collective-permute-start.2
  70.8 1.9 %collective-permute-done.2 = f32[1280,128]{0,1:T(8,128)} collective-permute-done((f32[1280,128]{0,1:T(8,128)S(1)}, f32[1280,128]{0,1:T(8,128)}, u32[]{:S(2)}, u32[]{:S(2)}) %collective-permute-start.2) | collective-permute-done | bytes 655392 | tf_op jit(solution)/shard_map/ppermute | solution.py:44
  72.7 1.2 bitcast_add_fusion
  74.1 23.2 %all_to_all.22 = f32[32,40,128]{2,1,0:T(8,128)S(1)} all-to-all(f32[32,40,128]{2,1,0:T(8,128)S(1)} %bitcast.66), channel_id=1, replica_groups=mesh['section'=4,'z'=8,'core'=2,'tensor'=4] {'z','tensor'}, dimensions={0} | all-to-all | bytes 1310720 | tf_op jit(solution)/shard_map/all_to_all | solution.py:74
  97.3 0.9 broadcast_in_dim.12
  98.2 5.6 %all-to-all-start.3 = ((f32[32,40,128]{2,1,0:T(8,128)}), f32[32,40,128]{2,1,0:T(8,128)S(1)}, u32[]{:S(2)}, u32[]{:S(2)}) async-start(f32[32,40,128]{2,1,0:T(8,128)} %broadcast_in_dim.12), calls=%async_computation.3 | async-start | bytes 1310720 | tf_op jit(solution)/shard_map/all_to_all | solution.py:75
  103.9 0.8 multiply_reduce_fusion
  104.7 16.6 %all-to-all-done.3 = f32[32,40,128]{2,1,0:T(8,128)S(1)} async-done(((f32[32,40,128]{2,1,0:T(8,128)}), f32[32,40,128]{2,1,0:T(8,128)S(1)}, u32[]{:S(2)}, u32[]{:S(2)}) %all-to-all-start.3) | async-done | bytes 655392 | tf_op jit(solution)/shard_map/all_to_all | solution.py:75
  121.4 3.6 %collective-permute-start.3 = (f32[1280,128]{1,0:T(8,128)S(1)}, f32[1280,128]{1,0:T(8,128)S(1)}, u32[]{:S(2)}, u32[]{:S(2)}) collective-permute-start(f32[1280,128]{1,0:T(8,128)S(1)} %bitcast.67), channel_id=1, source_target_pairs={{0,4},{4,0},{1,5},{5,1},{2,6},{6,2},{3,7},{7,3},{8,12},{12,8},{9,1... | collective-permute-start | bytes 1966088 | tf_op jit(solution)/shard_map/ppermute | solution.py:44
  125.0 0.8 fusion.23
  125.8 0.9 collective-permute-done.3
  126.7 1.8 %select_reduce_fusion = (f32[]{:T(128)}, f32[256,256]{1,0:T(8,128)S(1)}) fusion(f32[1280,128]{1,0:T(8,128)S(1)} %collective-permute-done.3, f32[1280,128]{1,0:T(8,128)S(1)} %bitcast.68, pred[]{:T(512)S(6)} %eq.20), kind=kOutput, calls=%fused_computation.30 | convolution fusion | flops 504496128 | bytes 1572869 | tf_op jit(solution)/shard_map/dot_general | solution.py:16
  129.2 0.3 fusion.14
  129.5 0.4 fusion.13
  129.9 0.3 fusion.16
  130.2 0.3 fusion.12
  130.5 0.4 fusion.15
  131.2 0.4 fusion.17
  131.9 0.4 fusion.6
  132.3 0.3 fusion.19
  132.6 0.3 fusion.11
  133.2 1.7 %convolution_bitcast_fusion = f32[1,1280,256]{2,1,0:T(8,128)} fusion(f32[256,256]{1,0:T(8,128)S(1)} %convolution_multiply_fusion.1, f32[1280,128]{1,0:T(8,128)S(1)} %collective-permute-done.3, f32[1280,128]{1,0:T(8,128)S(1)} %bitcast.69, pred[]{:T(512)S(6)} %eq.20), kind=kOutput, calls=%fused_computation.2 | convolution fusion | flops 504299520 | bytes 2883585 | tf_op jit(solution)/shard_map/dot_general | solution.py:12
  (25 shorter events, 1.6 us)
Async XLA Ops:
  0.6 1.3 copy-start
  7.8 5.1 %collective-permute-start = (f32[8,80,256]{2,1,0:T(8,128)}, f32[8,80,256]{2,1,0:T(8,128)S(1)}, u32[]{:S(2)}, u32[]{:S(2)}) collective-permute-start(f32[8,80,256]{2,1,0:T(8,128)} %dynamic-slice_bitcast_fusion.1), channel_id=1, source_target_pairs={{0,4},{4,0},{1,5},{5,1},{2,6},{6,2},{3,7},{7,3},{8,12},{12,8},{9,1... | collective-permute-start | bytes 1966088 | tf_op jit(solution)/shard_map/ppermute | solution.py:44
  59.5 4.8 %collective-permute-start.1 = (f32[8,80,256]{2,1,0:T(8,128)S(1)}, f32[8,80,256]{2,1,0:T(8,128)S(1)}, u32[]{:S(2)}, u32[]{:S(2)}) collective-permute-start(f32[8,80,256]{2,1,0:T(8,128)S(1)} %all_to_all.21), channel_id=1, source_target_pairs={{0,4},{4,0},{1,5},{5,1},{2,6},{6,2},{3,7},{7,3},{8,12},{12,8},{9,1... | collective-permute-start | bytes 1966088 | tf_op jit(solution)/shard_map/ppermute | solution.py:44
  70.4 2.3 %collective-permute-start.2 = (f32[1280,128]{0,1:T(8,128)S(1)}, f32[1280,128]{0,1:T(8,128)}, u32[]{:S(2)}, u32[]{:S(2)}) collective-permute-start(f32[1280,128]{0,1:T(8,128)S(1)} %dynamic-slice_bitcast_fusion), channel_id=1, source_target_pairs={{0,4},{4,0},{1,5},{5,1},{2,6},{6,2},{3,7},{7,3},{8,12},{12,8},{9,1... | collective-permute-start | bytes 1966088 | tf_op jit(solution)/shard_map/ppermute | solution.py:44
  97.3 6.5 %copy-start.4 = (f32[1,1,80,256]{3,2,1,0:T(8,128)S(1)}, f32[1,1,80,256]{3,2,1,0:T(8,128)}, u32[]{:S(2)}) copy-start(f32[1,1,80,256]{3,2,1,0:T(8,128)} %param.9) | copy-start | bytes 245764
  97.3 6.6 %copy-start.5 = (f32[1,1,80,256]{3,2,1,0:T(8,128)S(1)}, f32[1,1,80,256]{3,2,1,0:T(8,128)}, u32[]{:S(2)}) copy-start(f32[1,1,80,256]{3,2,1,0:T(8,128)} %param.8) | copy-start | bytes 245764
  97.3 6.6 %copy-start.3 = (bf16[1,1,80,1280]{3,2,1,0:T(8,128)(2,1)S(1)}, bf16[1,1,80,1280]{3,2,1,0:T(8,128)(2,1)}, u32[]{:S(2)}) copy-start(bf16[1,1,80,1280]{3,2,1,0:T(8,128)(2,1)} %param.6) | copy-start | bytes 614404
  98.2 23.2 %all-to-all-start.3 = ((f32[32,40,128]{2,1,0:T(8,128)}), f32[32,40,128]{2,1,0:T(8,128)S(1)}, u32[]{:S(2)}, u32[]{:S(2)}) async-start(f32[32,40,128]{2,1,0:T(8,128)} %broadcast_in_dim.12), calls=%async_computation.3 | async-start | bytes 1310720 | tf_op jit(solution)/shard_map/all_to_all | solution.py:75
  103.9 21.9 %copy-start.1 = (f32[1,1,80,256]{3,2,1,0:T(8,128)}, f32[1,1,80,256]{3,2,1,0:T(8,128)S(1)}, u32[]{:S(2)}) copy-start(f32[1,1,80,256]{3,2,1,0:T(8,128)S(1)} %get-tuple-element.6) | copy-start | bytes 245764
  103.9 21.9 %copy-start.2 = (f32[1,1,80,256]{3,2,1,0:T(8,128)}, f32[1,1,80,256]{3,2,1,0:T(8,128)S(1)}, u32[]{:S(2)}) copy-start(f32[1,1,80,256]{3,2,1,0:T(8,128)S(1)} %get-tuple-element.7) | copy-start | bytes 245764
  121.4 5.3 %collective-permute-start.3 = (f32[1280,128]{1,0:T(8,128)S(1)}, f32[1280,128]{1,0:T(8,128)S(1)}, u32[]{:S(2)}, u32[]{:S(2)}) collective-permute-start(f32[1280,128]{1,0:T(8,128)S(1)} %bitcast.67), channel_id=1, source_target_pairs={{0,4},{4,0},{1,5},{5,1},{2,6},{6,2},{3,7},{7,3},{8,12},{12,8},{9,1... | collective-permute-start | bytes 1966088 | tf_op jit(solution)/shard_map/ppermute | solution.py:44
